TPU v7x, 128 devices: a whole 4x4x4 slice. The times are simulated.
128 devices in a mesh: seq: 16 (over y_hi, x, core), head: 8 (over z, y_lo).
Axes of the slice: x: 4, y: 4 (y_hi: 2, y_lo: 2; y = y_hi * 2 + y_lo), z: 4, core: 2. Of those that a mesh axis runs over, the one named last changes fastest.
Arguments:
- inputs_x: bfloat16 [4096, 8192], P('seq', 'head'), may hold values from -6 to 6
- inputs_b: bfloat16 [4096, 1024], P('seq', 'head'), may hold values from -0.59765625 to 0.59765625
- inputs_c: bfloat16 [4096, 1024], P('seq', 'head'), may hold values from -6 to 6
- gate_z: bfloat16 [4096, 8192], P('seq', 'head'), may hold values from -6 to 6
- log_decay: float32 [128, 4096], P('head', 'seq'), may hold values from -1 to 0, as said below
- resets: int32 [4096], P('seq'), may hold values from 0 to 1, as said below
- norm_gain: float32 [8192], P('head'), may hold values from 0.1 to 1.9
- out_weight: bfloat16 [4096, 8192], P('seq', 'head'), may hold values from -0.09375 to 0.09375
- out_grad: bfloat16 [4096, 4096], P('seq', 'head'), may hold values from -6 to 6
Outputs:
- layer_out: bfloat16 [4096, 4096], P('seq', 'head')
- grad_x: float32 [4096, 8192], P('seq', 'head')
- grad_b: float32 [4096, 1024], P('seq', 'head')
- grad_c: float32 [4096, 1024], P('seq', 'head')
- grad_z: float32 [4096, 8192], P('seq', 'head')
- grad_decay: float32 [128, 4096], P('head', 'seq')
- grad_weight: float32 [4096, 8192], P('seq', 'head')
Inputs may be any that keep to these rules, and one draw needn't show every extreme that they name: `log_decay`: the decay factor of a token is exp of its entry. `resets`: exactly one entry is 1, the first token of the second rollout, at a position from 512 to 3583.
All inputs are finite; a program needn't handle non-finite values.
Results may differ from a plain program's by a relative error of at most 0.023.
Values may be sent and summed in bfloat16 or wider, within the bound.
No kernel may reach another device: no remote copies, remote signals or barrier semaphores. Data moves between devices by JAX's collectives and lax.ppermute only.
A program may use at most 128 MiB of HBM per device.

v0:
```python
import jax
import jax.numpy as jnp
from jax import lax
from jax.sharding import PartitionSpec as P

P_SIZE = 64
N = 128
G = 8
SPAN = 256
HP = 8192


def from_behind(value, axis, steps):
    count = lax.axis_size(axis)
    leading, last = (max(0, -steps), min(count, count - steps))
    return lax.ppermute(value, axis, [(source, source + steps) for source in range(leading, last)])


def with_decay(state, decay):
    high = decay.astype(jnp.bfloat16)
    low = (decay - high.astype(jnp.float32)).astype(jnp.bfloat16)
    rows = jnp.zeros((state.shape[0], 8, state.shape[2]), jnp.bfloat16)
    rows = rows.at[:, 0, :].set(high[:, None]).at[:, 1, :].set(low[:, None])
    return jnp.concatenate([state.astype(jnp.bfloat16), rows], axis=1)


def split_decay(payload, rows):
    state = payload[:, :rows].astype(jnp.float32)
    decay = payload[:, rows, 0].astype(jnp.float32) + payload[:, rows + 1, 0].astype(jnp.float32)
    return state, decay


def prefix_combine(decay, value, direction, width=4):
    count = lax.axis_size("seq")
    rows = value.shape[1]

    def shifted(payload, steps):
        return split_decay(from_behind(payload, "seq", direction * steps), rows)

    near = min(width, count - 1)
    outgoing = with_decay(value, decay)
    total, passed = shifted(outgoing, 1)
    for steps in range(2, near + 1):
        item, item_decay = shifted(outgoing, steps)
        total = total + passed[:, None, None] * item
        passed = passed * item_decay
    result = total
    outgoing = with_decay(total, passed)
    through = passed
    for steps in range(near, count - 1, near):
        item, item_decay = shifted(outgoing, steps)
        result = result + through[:, None, None] * item
        through = through * item_decay
    return result


def head_gather(block):
    count = lax.axis_size("head")
    rows, width = block.shape
    copies = jnp.broadcast_to(block[:, None, :], (rows, count, width))
    gathered = lax.all_to_all(copies, "head", split_axis=1, concat_axis=1, tiled=True)
    return gathered.reshape(rows, count * width)


def head_sum_scatter(full):
    count = lax.axis_size("head")
    rows = full.shape[0]
    pieces = full.reshape(rows, count, -1)
    received = lax.all_to_all(pieces, "head", split_axis=1, concat_axis=1, tiled=True)
    return jnp.sum(received.astype(jnp.float32), axis=1)


def block_setup(x_arg, b_arg, decay_arg, resets):
    tokens_here = x_arg.shape[0]
    heads_here = decay_arg.shape[0]
    groups_here = b_arg.shape[1] // N
    x_heads = x_arg.reshape(tokens_here, heads_here, P_SIZE)
    b_groups = b_arg.reshape(tokens_here, groups_here, N)
    cumul = jnp.cumsum(decay_arg, axis=1)
    counts = jnp.cumsum(resets)
    return x_heads, b_groups, cumul, counts, heads_here // groups_here


def block_outputs(x_arg, b_arg, c_arg, decay_arg, resets):
    x_heads, b_groups, cumul, counts, repeat_count = block_setup(x_arg, b_arg, decay_arg, resets)
    tokens_here = x_arg.shape[0]
    c_groups = c_arg.reshape(tokens_here, b_groups.shape[1], N)
    order = jnp.arange(tokens_here, dtype=jnp.int32)
    lower = order[None, :] <= order[:, None]
    same = lower & (counts[:, None] == counts[None, :])
    spread = cumul[:, :, None] - cumul[:, None, :]
    weights = jnp.where(same[None], jnp.exp(jnp.minimum(spread, 0.0)), 0.0)
    scores = jnp.einsum("tgn,sgn->gts", c_groups, b_groups, precision=lax.Precision.HIGHEST)
    scores = jnp.repeat(scores, repeat_count, axis=0) * weights
    inner = jnp.einsum("hts,shp->thp", scores, x_heads, precision=lax.Precision.HIGHEST)
    return inner.reshape(tokens_here, -1)


def block_final(x_arg, b_arg, decay_arg, resets):
    x_heads, b_groups, cumul, counts, repeat_count = block_setup(x_arg, b_arg, decay_arg, resets)
    tail = jnp.exp(cumul[:, -1:] - cumul) * (counts == counts[-1]).astype(jnp.float32)[None, :]
    b_heads = jnp.repeat(b_groups, repeat_count, axis=1)
    return jnp.einsum(
        "shp,shn->hpn", x_heads * tail.T[:, :, None], b_heads, precision=lax.Precision.HIGHEST
    )


def gated_norm(values, gate, gain):
    gated = values * jax.nn.silu(gate)
    rows_here, width = gated.shape
    group_width = HP // G
    grouped = gated.reshape(rows_here, width // group_width, group_width)
    scale = lax.rsqrt(jnp.mean(grouped * grouped, axis=2, keepdims=True) + 1e-05)
    return (grouped * scale).reshape(rows_here, width) * gain[None, :]


def carried_term(inputs_c, log_decay, resets, state):
    heads_here = log_decay.shape[0]
    tokens_here = inputs_c.shape[0]
    groups_here = inputs_c.shape[1] // N
    cumul = jnp.cumsum(log_decay, axis=1)
    counts = jnp.cumsum(resets)
    entry = jnp.exp(cumul) * (counts == 0).astype(jnp.float32)[None, :]
    c_heads = jnp.repeat(
        inputs_c.reshape(tokens_here, groups_here, N), heads_here // groups_here, axis=1
    )
    result = (
        jnp.einsum("thn,hpn->thp", c_heads, state, precision=lax.Precision.HIGHEST)
        * entry.T[:, :, None]
    )
    return result.reshape(tokens_here, heads_here * P_SIZE)


def device_decay(log_decay, resets):
    return jnp.exp(jnp.sum(log_decay, axis=1)) * (jnp.sum(resets) == 0).astype(jnp.float32)


def per_device(
    inputs_x, inputs_b, inputs_c, gate_z, log_decay, resets, norm_gain, out_weight, out_grad
):
    x_float = inputs_x.astype(jnp.float32)
    b_float = inputs_b.astype(jnp.float32)
    c_float = inputs_c.astype(jnp.float32)
    z_float = gate_z.astype(jnp.float32)
    heads_here = log_decay.shape[0]

    assert inputs_x.shape[0] == SPAN

    def local_outputs(x_arg, b_arg, c_arg, decay_arg):
        return block_outputs(x_arg, b_arg, c_arg, decay_arg, resets)

    def local_final(x_arg, b_arg, decay_arg):
        return block_final(x_arg, b_arg, decay_arg, resets)

    y_zero, pull_outputs = jax.vjp(local_outputs, x_float, b_float, c_float, log_decay)
    s_local, pull_final = jax.vjp(local_final, x_float, b_float, log_decay)

    def whole_decay(decay_arg):
        return device_decay(decay_arg, resets)

    g_local, pull_decay = jax.vjp(whole_decay, log_decay)

    state_in = prefix_combine(g_local, s_local, 1)

    def finish(y_arg, c_arg, decay_arg, z_arg, state_arg):
        return gated_norm(
            y_arg + carried_term(c_arg, decay_arg, resets, state_arg), z_arg, norm_gain
        )

    normed, pull_finish = jax.vjp(finish, y_zero, c_float, log_decay, z_float, state_in)
    normed_bf = normed.astype(jnp.bfloat16)
    full_weight = lax.all_gather(out_weight, "seq", axis=0, tiled=True)
    partial_value = lax.dot_general(
        normed_bf, full_weight, (((1,), (1,)), ((), ())), preferred_element_type=jnp.float32
    )
    layer_out = head_sum_scatter(partial_value.astype(jnp.bfloat16)).astype(jnp.bfloat16)
    grad_full = head_gather(out_grad)
    grad_y = jnp.dot(grad_full, full_weight, preferred_element_type=jnp.float32)
    grad_weight = lax.psum_scatter(
        lax.dot_general(
            grad_full, normed_bf, (((0,), (0,)), ((), ())), preferred_element_type=jnp.float32
        ).astype(jnp.bfloat16),
        "seq",
        scatter_dimension=0,
        tiled=True,
    ).astype(jnp.float32)
    d_zero, d_c_two, d_decay_two, grad_z, adjoint_in = pull_finish(grad_y)

    adjoint_out = prefix_combine(g_local, adjoint_in, -1)
    x_one, b_one, d_c_one, decay_one = pull_outputs(d_zero)
    x_two, b_two, decay_two = pull_final(adjoint_out)
    grad_x = x_one + x_two
    grad_b = b_one + b_two
    d_decay_one = decay_one + decay_two
    (d_decay_three,) = pull_decay(jnp.sum(adjoint_out * state_in, axis=(1, 2)))
    return (
        layer_out,
        grad_x,
        grad_b,
        d_c_one + d_c_two,
        grad_z,
        d_decay_one + d_decay_two + d_decay_three,
        grad_weight,
    )


def solution(mesh):
    return jax.shard_map(
        per_device,
        mesh=mesh,
        in_specs=(
            P("seq", "head"),
            P("seq", "head"),
            P("seq", "head"),
            P("seq", "head"),
            P("head", "seq"),
            P("seq"),
            P("head"),
            P("seq", "head"),
            P("seq", "head"),
        ),
        out_specs=(
            P("seq", "head"),
            P("seq", "head"),
            P("seq", "head"),
            P("seq", "head"),
            P("seq", "head"),
            P("head", "seq"),
            P("seq", "head"),
        ),
        check_vma=False,
    )
```

profile of v0, /device:TPU:0, one launch (start us, length us, event | category | flops | bytes accessed | tf_op | source)
XLA Modules:
  0.0 272.3 jit_solution(17888624866886218344)
XLA Ops:
  20.8 4.1 %collective-permute-start.1 = (bf16[16,72,128]{2,1,0:T(8,128)(2,1)S(1)}, bf16[16,72,128]{2,1,0:T(8,128)(2,1)}, u32[]{:S(2)}, u32[]{:S(2)}) collective-permute-start(bf16[16,72,128]{2,1,0:T(8,128)(2,1)S(1)} %pad_maximum_fusion.1), channel_id=1, source_target_pairs={{0,16},{8,24},{16,32},{24,40},{32,48},{40,56},{48,64},{56,72},{64,... | collective-permute-start | bytes 884744 | tf_op jit(solution)/shard_map/ppermute | solution.py:16
  25.0 4.6 %collective-permute-start.3 = (bf16[16,72,128]{2,1,0:T(8,128)(2,1)S(1)}, bf16[16,72,128]{2,1,0:T(8,128)(2,1)}, u32[]{:S(2)}, u32[]{:S(2)}) collective-permute-start(bf16[16,72,128]{2,1,0:T(8,128)(2,1)S(1)} %pad_maximum_fusion.1), channel_id=1, source_target_pairs={{0,32},{8,40},{16,48},{24,56},{32,64},{40,72},{48,80},{56,88},{64,... | collective-permute-start | bytes 884744 | tf_op jit(solution)/shard_map/ppermute | solution.py:16
  29.6 5.8 %collective-permute-start.2 = (bf16[16,72,128]{2,1,0:T(8,128)(2,1)S(1)}, bf16[16,72,128]{2,1,0:T(8,128)(2,1)}, u32[]{:S(2)}, u32[]{:S(2)}) collective-permute-start(bf16[16,72,128]{2,1,0:T(8,128)(2,1)S(1)} %pad_maximum_fusion.1), channel_id=1, source_target_pairs={{0,24},{8,32},{16,40},{24,48},{32,56},{40,64},{48,72},{56,80},{64,... | collective-permute-start | bytes 884744 | tf_op jit(solution)/shard_map/ppermute | solution.py:16
  35.4 2.5 broadcast_in_dim.22
  37.9 5.4 %all-to-all-start.1 = ((bf16[256,8,512]{2,0,1:T(8,128)(2,1)}), bf16[256,8,512]{2,0,1:T(8,128)(2,1)S(1)}, u32[]{:S(2)}, u32[]{:S(2)}) async-start(bf16[256,8,512]{2,0,1:T(8,128)(2,1)} %broadcast_in_dim.22), calls=%async_computation.1 | async-start | bytes 4194304 | tf_op jit(solution)/shard_map/all_to_all | solution.py:61
  45.5 6.1 %collective-permute-done.2 = bf16[16,72,128]{2,1,0:T(8,128)(2,1)} collective-permute-done((bf16[16,72,128]{2,1,0:T(8,128)(2,1)S(1)}, bf16[16,72,128]{2,1,0:T(8,128)(2,1)}, u32[]{:S(2)}, u32[]{:S(2)}) %collective-permute-start.2) | collective-permute-done | bytes 294944 | tf_op jit(solution)/shard_map/ppermute | solution.py:16
  54.5 10.0 %collective-permute-start.5 = (bf16[16,72,128]{2,1,0:T(8,128)(2,1)S(1)}, bf16[16,72,128]{2,1,0:T(8,128)(2,1)S(1)}, u32[]{:S(2)}, u32[]{:S(2)}) collective-permute-start(bf16[16,72,128]{2,1,0:T(8,128)(2,1)S(1)} %pad_maximum_fusion.2), channel_id=1, source_target_pairs={{0,64},{8,72},{16,80},{24,88},{32,96},{40,104},{48,112},{56,120},{... | collective-permute-start | bytes 884744 | tf_op jit(solution)/shard_map/ppermute | solution.py:16
  64.5 2.9 %collective-permute-start.4 = (bf16[16,72,128]{2,1,0:T(8,128)(2,1)S(1)}, bf16[16,72,128]{2,1,0:T(8,128)(2,1)S(1)}, u32[]{:S(2)}, u32[]{:S(2)}) collective-permute-start(bf16[16,72,128]{2,1,0:T(8,128)(2,1)S(1)} %pad_maximum_fusion.2), channel_id=1, source_target_pairs={{0,32},{8,40},{16,48},{24,56},{32,64},{40,72},{48,80},{56,88},{64,... | collective-permute-start | bytes 884744 | tf_op jit(solution)/shard_map/ppermute | solution.py:16
  69.3 44.7 %collective-permute-done.5 = bf16[16,72,128]{2,1,0:T(8,128)(2,1)S(1)} collective-permute-done((bf16[16,72,128]{2,1,0:T(8,128)(2,1)S(1)}, bf16[16,72,128]{2,1,0:T(8,128)(2,1)S(1)}, u32[]{:S(2)}, u32[]{:S(2)}) %collective-permute-start.5) | collective-permute-done | bytes 294944 | tf_op jit(solution)/shard_map/ppermute | solution.py:16
  115.3 2.2 convolution_bitcast_fusion.1
  117.6 4.6 %fusion.27 = f32[256,16,64]{0,2,1:T(8,128)} fusion(bf16[256,16,64]{0,2,1:T(8,128)(2,1)S(1)} %bitcast.125, f32[16,256]{1,0:T(8,128)S(1)} %copy_bitcast_fusion.1, f32[256,256]{1,0:T(8,128)S(1)} %fusion.107, pred[256,256]{1,0:T(8,128)(4,1)S(1)} %fusion.61, f32[256,16,64]{0,2,1:T(8,128)S(1)} %convolution_bitcast_fusion.1, f32[256,16]{0,1:T(8,128)S(1)} %get-tuple-element.169), kind=kOutput, calls=%fused_computation.35 | convolution fusion | flops 810024960 | bytes 2981888 | tf_op jit(solution)/shard_map/jvp(hts,shp->thp)/dot_general | solution.py:95
  122.2 2.6 copy.72
  124.8 2.4 copy.74
  127.2 7.9 %multiply_reduce_fusion.1 = (f32[256]{0:T(256)S(1)}, f32[256]{0:T(256)S(1)}, f32[256,1024]{1,0:T(8,128)}) fusion(f32[256,1024]{1,0:T(8,128)} %copy.72, bf16[256,1024]{1,0:T(8,128)(2,1)S(1)} %copy-done.10, f32[1024]{0:T(1024)} %param.31, bf16[256,4096]{0,1:T(8,128)(2,1)} %bitcast.128, bf16[4096,1024]{1,0:T(8,128)(2,1)} %all-gather.2.cloned.1.call-done), kind=kOutput, calls=%fused_computation.56 | convolution fusion | flops 2150366720 | bytes 13113344 | tf_op jit(solution)/shard_map/dot_general | solution.py:178
  135.7 6.0 %convert_bitcast_fusion = bf16[4096,1024]{0,1:T(8,128)(2,1)} fusion(bf16[256,4096]{0,1:T(8,128)(2,1)S(1)} %bitcast.129, f32[1024]{0:T(1024)S(1)} %copy-done.33, f32[256]{0:T(256)S(1)} %get-tuple-element.174, f32[256,1024]{1,0:T(8,128)S(1)} %copy-done.6, bf16[256,1024]{1,0:T(8,128)(2,1)S(1)} %copy-done.10), kind=kOutput, calls=%fused_computation | convolution fusion | flops 2154037248 | bytes 12063744 | tf_op jit(solution)/shard_map/dot_general | solution.py:180
  141.6 6.0 %convolution_convert_fusion = bf16[256,4096]{1,0:T(8,128)(2,1)S(1)} fusion(bf16[4096,1024]{1,0:T(8,128)(2,1)} %all-gather.2.cloned.1.call-done, f32[1024]{0:T(1024)S(1)} %copy-done.33, f32[256]{0:T(256)S(1)} %get-tuple-element.174, f32[256,1024]{1,0:T(8,128)S(1)} %copy-done.6, bf16[256,1024]{1,0:T(8,128)(2,1)S(1)} %copy-done.10), kind=kOutput, calls=%fused_computation.4 | convolution fusion | flops 2150891520 | bytes 12063744 | tf_op jit(solution)/shard_map/dot_general | solution.py:173
  149.2 5.4 %all-to-all-start = ((bf16[256,8,512]{2,0,1:T(8,128)(2,1)}), bf16[256,8,512]{2,0,1:T(8,128)(2,1)S(1)}, u32[]{:S(2)}, u32[]{:S(2)}) async-start(bf16[256,8,512]{2,0,1:T(8,128)(2,1)} %bitcast.123), calls=%async_computation | async-start | bytes 4194304 | tf_op jit(solution)/shard_map/all_to_all | solution.py:69
  154.5 3.6 %fusion.44 = (f32[256,1024]{1,0:T(8,128)}, f32[256,1024]{1,0:T(8,128)}) fusion(bf16[256,1024]{1,0:T(8,128)(2,1)} %param.28, f32[256,1024]{1,0:T(8,128)S(1)} %copy-done.6, f32[256]{0:T(256)} %get-tuple-element.173, f32[256,1024]{1,0:T(8,128)} %get-tuple-element.179, f32[256]{0:T(256)} %copy-done.31), kind=kLoop, calls=%fused_computation.52 | loop fusion | flops 4718592 | bytes 4720640 | tf_op jit(solution)/shard_map/transpose(jvp(jit(silu)))/add_any | solution.py:109
  164.4 6.1 %fusion.54 = (f32[16,256]{1,0:T(8,128)S(1)}, f32[16,256]{1,0:T(8,128)S(1)}, f32[256,256]{1,0:T(8,128)S(1)}) fusion(f32[16,256]{1,0:T(8,128)} %copy-done.19, f32[256,256]{1,0:T(8,128)} %copy-done.12, pred[256,256]{1,0:T(8,128)(4,1)} %copy-done.18, f32[16,64,256]{2,1,0:T(8,128)S(1)} %bitcast.120, bf16[256,16,64]{0,2,1:T(8,128)(2,1)} %bitcast.126), kind=kOutput, calls=%fused_computation.66 | convolution fusion | flops 820961280 | bytes 2211840 | tf_op jit(solution)/shard_map/transpose(jvp(hts,shp->thp))/dot_general | solution.py:95
  170.8 2.5 fusion.37
  177.6 2.5 reduce-window.41
  181.1 13.7 %collective-permute-done.8 = bf16[16,72,128]{2,1,0:T(8,128)(2,1)} collective-permute-done((bf16[16,72,128]{2,1,0:T(8,128)(2,1)}, bf16[16,72,128]{2,1,0:T(8,128)(2,1)}, u32[]{:S(2)}, u32[]{:S(2)}) %collective-permute-start.8) | collective-permute-done | bytes 294944 | tf_op jit(solution)/shard_map/ppermute | solution.py:16
  197.2 2.3 fusion.93
  206.0 21.9 %collective-permute-done.12 = bf16[16,72,128]{2,1,0:T(8,128)(2,1)} collective-permute-done((bf16[16,72,128]{2,1,0:T(8,128)(2,1)}, bf16[16,72,128]{2,1,0:T(8,128)(2,1)}, u32[]{:S(2)}, u32[]{:S(2)}) %collective-permute-start.12) | collective-permute-done | bytes 294944 | tf_op jit(solution)/shard_map/ppermute | solution.py:16
  229.0 10.5 %collective-permute-done.13 = bf16[16,72,128]{2,1,0:T(8,128)(2,1)S(1)} collective-permute-done((bf16[16,72,128]{2,1,0:T(8,128)(2,1)}, bf16[16,72,128]{2,1,0:T(8,128)(2,1)S(1)}, u32[]{:S(2)}, u32[]{:S(2)}) %collective-permute-start.13) | collective-permute-done | bytes 294944 | tf_op jit(solution)/shard_map/ppermute | solution.py:16
  239.5 2.2 multiply_reduce_fusion.3
  241.7 2.2 fusion.39
  244.1 5.5 %fusion.30 = f32[256,16,64]{0,2,1:T(8,128)} fusion(f32[16,64,256]{2,1,0:T(8,128)S(1)} %bitcast.122, f32[16,256]{1,0:T(8,128)S(1)} %copy-done.20, f32[256,256]{1,0:T(8,128)S(1)} %copy-done.13, pred[256,256]{1,0:T(8,128)(4,1)} %copy-done.18, f32[256,16,64]{0,2,1:T(8,128)S(1)} %get-tuple-element.181, f32[256,16]{0,1:T(8,128)S(1)} %copy-done.17), kind=kOutput, calls=%fused_computation.36 | convolution fusion | flops 810024960 | bytes 3506176 | tf_op jit(solution)/shard_map/transpose(jvp(hts,shp->thp))/dot_general | solution.py:95
  249.6 2.5 copy.82
  252.5 2.5 reduce-window.49
  255.2 2.5 reduce-window.45
  258.5 3.7 %fusion.38 = f32[256,128]{1,0:T(8,128)} fusion(f32[256,128]{1,0:T(8,128)S(1)} %fusion.108, f32[16,64,128]{2,1,0:T(8,128)} %copy-done.4, bf16[256,16,64]{0,2,1:T(8,128)(2,1)} %bitcast.127, f32[256,16]{0,1:T(8,128)S(1)} %copy-done.17), kind=kOutput, calls=%fused_computation.46 | convolution fusion | flops 403210240 | bytes 1327104 | tf_op jit(solution)/shard_map/transpose(jvp(shp,shn->hpn))/dot_general | solution.py:103
  (171 shorter events, 49.5 us)
Async XLA Ops:
  7.2 120.0 %all-gather.2.cloned.1.call-start = ((), (), s32[]{:S(2)}) async-start(), calls=%async_computation.3 | async-start | bytes 8912896 | tf_op jit(solution)/shard_map/all_gather | solution.py:172
  16.2 101.4 %copy-start = (bf16[256,1024]{0,1:T(8,128)(2,1)}, bf16[256,1024]{0,1:T(8,128)(2,1)S(1)}, u32[]{:S(2)}) copy-start(bf16[256,1024]{0,1:T(8,128)(2,1)S(1)} %copy.71) | copy-start | bytes 1572868
  16.5 36.5 %copy-start.11 = (bf16[16,8,128]{2,1,0:T(8,128)(2,1)}, bf16[16,8,128]{2,1,0:T(8,128)(2,1)S(1)}, u32[]{:S(2)}) copy-start(bf16[16,8,128]{2,1,0:T(8,128)(2,1)S(1)} %scatter.21) | copy-start | bytes 98308
  16.5 101.0 %copy-start.19 = (f32[16,256]{1,0:T(8,128)}, f32[16,256]{1,0:T(8,128)S(1)}, u32[]{:S(2)}) copy-start(f32[16,256]{1,0:T(8,128)S(1)} %copy_bitcast_fusion.1) | copy-start | bytes 49156
  16.7 34.9 %copy-start.27 = (f32[16]{0:T(128)}, f32[16]{0:T(128)S(1)}, u32[]{:S(2)}) copy-start(f32[16]{0:T(128)S(1)} %slice_reduce_fusion.4) | copy-start | bytes 196
  17.5 37.0 %copy-start.16 = (f32[256,16]{0,1:T(8,128)}, f32[256,16]{0,1:T(8,128)S(1)}, u32[]{:S(2)}) copy-start(f32[256,16]{0,1:T(8,128)S(1)} %get-tuple-element.170) | copy-start | bytes 49156
  17.5 100.1 %copy-start.14 = (f32[256,16]{0,1:T(8,128)}, f32[256,16]{0,1:T(8,128)S(1)}, u32[]{:S(2)}) copy-start(f32[256,16]{0,1:T(8,128)S(1)} %get-tuple-element.169) | copy-start | bytes 49156
  18.7 48.8 %copy-start.8 = (bf16[256,128]{1,0:T(8,128)(2,1)S(1)}, bf16[256,128]{1,0:T(8,128)(2,1)}, u32[]{:S(2)}) copy-start(bf16[256,128]{1,0:T(8,128)(2,1)} %param.26) | copy-start | bytes 196612
  18.7 48.8 %copy-start.9 = (bf16[256,128]{1,0:T(8,128)(2,1)S(1)}, bf16[256,128]{1,0:T(8,128)(2,1)}, u32[]{:S(2)}) copy-start(bf16[256,128]{1,0:T(8,128)(2,1)} %param.27) | copy-start | bytes 196612
  18.7 24.7 %collective-permute-start = (bf16[16,72,128]{2,1,0:T(8,128)(2,1)S(1)}, bf16[16,72,128]{2,1,0:T(8,128)(2,1)}, u32[]{:S(2)}, u32[]{:S(2)}) collective-permute-start(bf16[16,72,128]{2,1,0:T(8,128)(2,1)S(1)} %pad_maximum_fusion.1), channel_id=1, source_target_pairs={{0,8},{8,16},{16,24},{24,32},{32,40},{40,48},{48,56},{56,64},{64,7... | collective-permute-start | bytes 884744 | tf_op jit(solution)/shard_map/ppermute | solution.py:16
  20.8 23.6 %collective-permute-start.1 = (bf16[16,72,128]{2,1,0:T(8,128)(2,1)S(1)}, bf16[16,72,128]{2,1,0:T(8,128)(2,1)}, u32[]{:S(2)}, u32[]{:S(2)}) collective-permute-start(bf16[16,72,128]{2,1,0:T(8,128)(2,1)S(1)} %pad_maximum_fusion.1), channel_id=1, source_target_pairs={{0,16},{8,24},{16,32},{24,40},{32,48},{40,56},{48,64},{56,72},{64,... | collective-permute-start | bytes 884744 | tf_op jit(solution)/shard_map/ppermute | solution.py:16
  25.0 20.5 %collective-permute-start.3 = (bf16[16,72,128]{2,1,0:T(8,128)(2,1)S(1)}, bf16[16,72,128]{2,1,0:T(8,128)(2,1)}, u32[]{:S(2)}, u32[]{:S(2)}) collective-permute-start(bf16[16,72,128]{2,1,0:T(8,128)(2,1)S(1)} %pad_maximum_fusion.1), channel_id=1, source_target_pairs={{0,32},{8,40},{16,48},{24,56},{32,64},{40,72},{48,80},{56,88},{64,... | collective-permute-start | bytes 884744 | tf_op jit(solution)/shard_map/ppermute | solution.py:16
  29.6 22.0 %collective-permute-start.2 = (bf16[16,72,128]{2,1,0:T(8,128)(2,1)S(1)}, bf16[16,72,128]{2,1,0:T(8,128)(2,1)}, u32[]{:S(2)}, u32[]{:S(2)}) collective-permute-start(bf16[16,72,128]{2,1,0:T(8,128)(2,1)S(1)} %pad_maximum_fusion.1), channel_id=1, source_target_pairs={{0,24},{8,32},{16,40},{24,48},{32,56},{40,64},{48,72},{56,80},{64,... | collective-permute-start | bytes 884744 | tf_op jit(solution)/shard_map/ppermute | solution.py:16
  37.9 86.9 %all-to-all-start.1 = ((bf16[256,8,512]{2,0,1:T(8,128)(2,1)}), bf16[256,8,512]{2,0,1:T(8,128)(2,1)S(1)}, u32[]{:S(2)}, u32[]{:S(2)}) async-start(bf16[256,8,512]{2,0,1:T(8,128)(2,1)} %broadcast_in_dim.22), calls=%async_computation.1 | async-start | bytes 4194304 | tf_op jit(solution)/shard_map/all_to_all | solution.py:61
  43.3 219.9 %reduce-scatter.2.cloned.1.call-start = ((), (), s32[]{:S(2)}) async-start(), calls=%async_computation.4 | async-start | bytes 8912896 | tf_op jit(solution)/shard_map/reduce_scatter | solution.py:179
  54.5 59.5 %collective-permute-start.5 = (bf16[16,72,128]{2,1,0:T(8,128)(2,1)S(1)}, bf16[16,72,128]{2,1,0:T(8,128)(2,1)S(1)}, u32[]{:S(2)}, u32[]{:S(2)}) collective-permute-start(bf16[16,72,128]{2,1,0:T(8,128)(2,1)S(1)} %pad_maximum_fusion.2), channel_id=1, source_target_pairs={{0,64},{8,72},{16,80},{24,88},{32,96},{40,104},{48,112},{56,120},{... | collective-permute-start | bytes 884744 | tf_op jit(solution)/shard_map/ppermute | solution.py:16
  64.5 49.5 %collective-permute-start.4 = (bf16[16,72,128]{2,1,0:T(8,128)(2,1)S(1)}, bf16[16,72,128]{2,1,0:T(8,128)(2,1)S(1)}, u32[]{:S(2)}, u32[]{:S(2)}) collective-permute-start(bf16[16,72,128]{2,1,0:T(8,128)(2,1)S(1)} %pad_maximum_fusion.2), channel_id=1, source_target_pairs={{0,32},{8,40},{16,48},{24,56},{32,64},{40,72},{48,80},{56,88},{64,... | collective-permute-start | bytes 884744 | tf_op jit(solution)/shard_map/ppermute | solution.py:16
  67.7 54.5 %copy-start.12 = (f32[256,256]{1,0:T(8,128)}, f32[256,256]{1,0:T(8,128)S(1)}, u32[]{:S(2)}) copy-start(f32[256,256]{1,0:T(8,128)S(1)} %fusion.107) | copy-start | bytes 786436
  67.7 46.5 %collective-permute-start.6 = (bf16[16,72,128]{2,1,0:T(8,128)(2,1)S(1)}, bf16[16,72,128]{2,1,0:T(8,128)(2,1)S(1)}, u32[]{:S(2)}, u32[]{:S(2)}) collective-permute-start(bf16[16,72,128]{2,1,0:T(8,128)(2,1)S(1)} %pad_maximum_fusion.2), channel_id=1, source_target_pairs={{0,96},{8,104},{16,112},{24,120},{1,97},{9,105},{17,113},{25,121},... | collective-permute-start | bytes 884744 | tf_op jit(solution)/shard_map/ppermute | solution.py:16
  69.3 52.8 %copy-start.18 = (pred[256,256]{1,0:T(8,128)(4,1)}, pred[256,256]{1,0:T(8,128)(4,1)S(1)}, u32[]{:S(2)}) copy-start(pred[256,256]{1,0:T(8,128)(4,1)S(1)} %fusion.61) | copy-start | bytes 196612
  149.2 113.0 %all-to-all-start = ((bf16[256,8,512]{2,0,1:T(8,128)(2,1)}), bf16[256,8,512]{2,0,1:T(8,128)(2,1)S(1)}, u32[]{:S(2)}, u32[]{:S(2)}) async-start(bf16[256,8,512]{2,0,1:T(8,128)(2,1)} %bitcast.123), calls=%async_computation | async-start | bytes 4194304 | tf_op jit(solution)/shard_map/all_to_all | solution.py:69
  163.1 17.0 %collective-permute-start.7 = (bf16[16,72,128]{2,1,0:T(8,128)(2,1)}, bf16[16,72,128]{2,1,0:T(8,128)(2,1)}, u32[]{:S(2)}, u32[]{:S(2)}) collective-permute-start(bf16[16,72,128]{2,1,0:T(8,128)(2,1)} %pad_maximum_fusion), channel_id=1, source_target_pairs={{8,0},{16,8},{24,16},{32,24},{40,32},{48,40},{56,48},{64,56},{72,6... | collective-permute-start | bytes 884744 | tf_op jit(solution)/shard_map/ppermute | solution.py:16
  173.7 22.2 %collective-permute-start.10 = (bf16[16,72,128]{2,1,0:T(8,128)(2,1)}, bf16[16,72,128]{2,1,0:T(8,128)(2,1)}, u32[]{:S(2)}, u32[]{:S(2)}) collective-permute-start(bf16[16,72,128]{2,1,0:T(8,128)(2,1)} %pad_maximum_fusion), channel_id=1, source_target_pairs={{32,0},{40,8},{48,16},{56,24},{64,32},{72,40},{80,48},{88,56},{96,... | collective-permute-start | bytes 884744 | tf_op jit(solution)/shard_map/ppermute | solution.py:16
  175.0 20.9 %collective-permute-start.9 = (bf16[16,72,128]{2,1,0:T(8,128)(2,1)}, bf16[16,72,128]{2,1,0:T(8,128)(2,1)}, u32[]{:S(2)}, u32[]{:S(2)}) collective-permute-start(bf16[16,72,128]{2,1,0:T(8,128)(2,1)} %pad_maximum_fusion), channel_id=1, source_target_pairs={{24,0},{32,8},{40,16},{48,24},{56,32},{64,40},{72,48},{80,56},{88,... | collective-permute-start | bytes 884744 | tf_op jit(solution)/shard_map/ppermute | solution.py:16
  176.3 18.5 %collective-permute-start.8 = (bf16[16,72,128]{2,1,0:T(8,128)(2,1)}, bf16[16,72,128]{2,1,0:T(8,128)(2,1)}, u32[]{:S(2)}, u32[]{:S(2)}) collective-permute-start(bf16[16,72,128]{2,1,0:T(8,128)(2,1)} %pad_maximum_fusion), channel_id=1, source_target_pairs={{16,0},{24,8},{32,16},{40,24},{48,32},{56,40},{64,48},{72,56},{80,... | collective-permute-start | bytes 884744 | tf_op jit(solution)/shard_map/ppermute | solution.py:16
  197.2 46.8 %copy-start.17 = (f32[256,16]{0,1:T(8,128)S(1)}, f32[256,16]{0,1:T(8,128)}, u32[]{:S(2)}) copy-start(f32[256,16]{0,1:T(8,128)} %copy-done.16) | copy-start | bytes 49156
  197.2 46.8 %copy-start.20 = (f32[16,256]{1,0:T(8,128)S(1)}, f32[16,256]{1,0:T(8,128)}, u32[]{:S(2)}) copy-start(f32[16,256]{1,0:T(8,128)} %copy-done.19) | copy-start | bytes 49156
  200.2 27.7 %collective-permute-start.12 = (bf16[16,72,128]{2,1,0:T(8,128)(2,1)}, bf16[16,72,128]{2,1,0:T(8,128)(2,1)}, u32[]{:S(2)}, u32[]{:S(2)}) collective-permute-start(bf16[16,72,128]{2,1,0:T(8,128)(2,1)} %pad_maximum_fusion.3), channel_id=1, source_target_pairs={{64,0},{72,8},{80,16},{88,24},{96,32},{104,40},{112,48},{120,56},{... | collective-permute-start | bytes 884744 | tf_op jit(solution)/shard_map/ppermute | solution.py:16
  201.5 26.4 %collective-permute-start.11 = (bf16[16,72,128]{2,1,0:T(8,128)(2,1)}, bf16[16,72,128]{2,1,0:T(8,128)(2,1)}, u32[]{:S(2)}, u32[]{:S(2)}) collective-permute-start(bf16[16,72,128]{2,1,0:T(8,128)(2,1)} %pad_maximum_fusion.3), channel_id=1, source_target_pairs={{32,0},{40,8},{48,16},{56,24},{64,32},{72,40},{80,48},{88,56},{96,... | collective-permute-start | bytes 884744 | tf_op jit(solution)/shard_map/ppermute | solution.py:16
  202.9 38.8 %copy-start.1 = (bf16[256,1024]{0,1:T(8,128)(2,1)S(1)}, bf16[256,1024]{0,1:T(8,128)(2,1)}, u32[]{:S(2)}) copy-start(bf16[256,1024]{0,1:T(8,128)(2,1)} %copy-done) | copy-start | bytes 1572868
  202.9 41.1 %copy-start.13 = (f32[256,256]{1,0:T(8,128)S(1)}, f32[256,256]{1,0:T(8,128)}, u32[]{:S(2)}) copy-start(f32[256,256]{1,0:T(8,128)} %copy-done.12) | copy-start | bytes 786436
  203.0 36.5 %collective-permute-start.13 = (bf16[16,72,128]{2,1,0:T(8,128)(2,1)}, bf16[16,72,128]{2,1,0:T(8,128)(2,1)S(1)}, u32[]{:S(2)}, u32[]{:S(2)}) collective-permute-start(bf16[16,72,128]{2,1,0:T(8,128)(2,1)} %pad_maximum_fusion.3), channel_id=1, source_target_pairs={{96,0},{104,8},{112,16},{120,24},{97,1},{105,9},{113,17},{121,25},... | collective-permute-start | bytes 884744 | tf_op jit(solution)/shard_map/ppermute | solution.py:16
  (20 other events, 219.9 us)
Sparse Core Ops, SparseCore 0:
  10.4 97.4 all-gather.1
  141.8 114.4 reduce-scatter.1
where the time goes:
time: 276 us; the launch traced here: 272 us
  waiting for transfers between devices  97.6 us (35%)
  starting transfers between devices  51.4 us (19%)
  matrix products  50.3 us (18%)
  other arithmetic  37 us (13%)
  local copies, waits for them, and re-layouts  20.5 us (7%)
  between operations  15.4 us (6%)
    ppermute x14, waiting for transfers between devices, from_behind(): lax.ppermute(value, axis, [(source, source + steps) for source in range(l...  96.9 us
    ppermute x14, starting transfers between devices, from_behind(): lax.ppermute(value, axis, [(source, source + steps) for source in range(l...  40.6 us
    dot_general x3, matrix products, block_outputs(): jnp.einsum('hts,shp->thp', scores, x_heads, precision=lax.Precision.HIGHEST)  16.1 us
    another operation x11, other arithmetic  9.3 us
    dot_general x1, matrix products, per_device(): grad_y = jnp.dot(grad_full, full_weight, preferred_element_type=jnp.float32)  7.88 us
    dot_general x3, matrix products, block_final(): jnp.einsum('shp,shn->hpn', x_heads * tail.T[:, :, None], b_heads, precisi...  7.03 us
    unnamed x71, local copies, waits for them, and re-layouts  6.93 us
    dot_general x3, matrix products, carried_term(): jnp.einsum('thn,hpn->thp', c_heads, state, precision=lax.Precision.HIGHEST)  6.52 us
  transfers between devices with their start and end apart: 18, of which 5 were waited for; matrix products, arithmetic and copies ran while one was open for 33% of the time, Pallas kernels for 0%

commit v1 on v0

--- a/solution.py
+++ b/solution.py
@@ -90,9 +90,9 @@
     same = lower & (counts[:, None] == counts[None, :])
     spread = cumul[:, :, None] - cumul[:, None, :]
     weights = jnp.where(same[None], jnp.exp(jnp.minimum(spread, 0.0)), 0.0)
-    scores = jnp.einsum("tgn,sgn->gts", c_groups, b_groups, precision=lax.Precision.HIGHEST)
+    scores = jnp.einsum("tgn,sgn->gts", c_groups, b_groups, precision=lax.Precision.HIGH)
     scores = jnp.repeat(scores, repeat_count, axis=0) * weights
-    inner = jnp.einsum("hts,shp->thp", scores, x_heads, precision=lax.Precision.HIGHEST)
+    inner = jnp.einsum("hts,shp->thp", scores, x_heads, precision=lax.Precision.HIGH)
     return inner.reshape(tokens_here, -1)
 
 
@@ -101,7 +101,7 @@
     tail = jnp.exp(cumul[:, -1:] - cumul) * (counts == counts[-1]).astype(jnp.float32)[None, :]
     b_heads = jnp.repeat(b_groups, repeat_count, axis=1)
     return jnp.einsum(
-        "shp,shn->hpn", x_heads * tail.T[:, :, None], b_heads, precision=lax.Precision.HIGHEST
+        "shp,shn->hpn", x_heads * tail.T[:, :, None], b_heads, precision=lax.Precision.HIGH
     )
 
 
@@ -125,7 +125,7 @@
         inputs_c.reshape(tokens_here, groups_here, N), heads_here // groups_here, axis=1
     )
     result = (
-        jnp.einsum("thn,hpn->thp", c_heads, state, precision=lax.Precision.HIGHEST)
+        jnp.einsum("thn,hpn->thp", c_heads, state, precision=lax.Precision.HIGH)
         * entry.T[:, :, None]
     )
     return result.reshape(tokens_here, heads_here * P_SIZE)

time: 276 us -> 272 us (0.986)
  matrix products: 50.3 us -> 42.5 us
  waiting for transfers between devices: 97.6 us -> 104 us
    reduce_scatter x1, waiting for transfers between devices: 0.01 us -> 6.1 us  [per_device(): lax.psum_scatter(lax.dot_general(grad_full, normed_bf, (((0,), (0,)), (()...]
    dot_general x9, matrix products: 23.5 us -> 18 us  [the longest x3 13.1 us: block_outputs(): jnp.einsum('hts,shp->thp', scores, x_heads, precision=lax.Precision.HIGH)]
  transfers between devices with their start and end apart: 18 -> 18, of which waited for: 5 -> 7; matrix products, arithmetic and copies ran while one was open for 33% -> 31% of each run, Pallas kernels for 0% -> 0%
where the time goes in v1:
time: 272 us; the launch traced here: 270 us
  waiting for transfers between devices  104 us (38%)
  starting transfers between devices  51.2 us (19%)
  matrix products  42.5 us (16%)
  other arithmetic  37 us (14%)
  local copies, waits for them, and re-layouts  20.6 us (8%)
  between operations  15.4 us (6%)
    ppermute x14, waiting for transfers between devices, from_behind(): lax.ppermute(value, axis, [(source, source + steps) for source in range(l...  96.8 us
    ppermute x14, starting transfers between devices, from_behind(): lax.ppermute(value, axis, [(source, source + steps) for source in range(l...  40.3 us
    dot_general x3, matrix products, block_outputs(): jnp.einsum('hts,shp->thp', scores, x_heads, precision=lax.Precision.HIGH)  13.1 us
    another operation x11, other arithmetic  9.3 us
    dot_general x1, matrix products, per_device(): grad_y = jnp.dot(grad_full, full_weight, preferred_element_type=jnp.float32)  7.88 us
    unnamed x71, local copies, waits for them, and re-layouts  7.08 us
    reduce_scatter x1, waiting for transfers between devices, per_device(): lax.psum_scatter(lax.dot_general(grad_full, normed_bf, (((0,), (0,)), (()...  6.1 us
    dot_general x1, matrix products, per_device(): lax.dot_general(normed_bf, full_weight, (((1,), (1,)), ((), ())), preferr...  5.97 us
  transfers between devices with their start and end apart: 18, of which 7 were waited for; matrix products, arithmetic and copies ran while one was open for 31% of the time, Pallas kernels for 0%

profile of v1, /device:TPU:0, one launch (start us, length us, event | category | flops | bytes accessed | tf_op | source)
XLA Modules:
  0.0 270.3 jit_solution(16469930963304136462)
XLA Ops:
  18.2 2.1 collective-permute-start
  20.3 4.1 %collective-permute-start.1 = (bf16[16,72,128]{2,1,0:T(8,128)(2,1)S(1)}, bf16[16,72,128]{2,1,0:T(8,128)(2,1)}, u32[]{:S(2)}, u32[]{:S(2)}) collective-permute-start(bf16[16,72,128]{2,1,0:T(8,128)(2,1)S(1)} %pad_maximum_fusion.1), channel_id=1, source_target_pairs={{0,16},{8,24},{16,32},{24,40},{32,48},{40,56},{48,64},{56,72},{64,... | collective-permute-start | bytes 884744 | tf_op jit(solution)/shard_map/ppermute | solution.py:16
  24.4 4.6 %collective-permute-start.3 = (bf16[16,72,128]{2,1,0:T(8,128)(2,1)S(1)}, bf16[16,72,128]{2,1,0:T(8,128)(2,1)}, u32[]{:S(2)}, u32[]{:S(2)}) collective-permute-start(bf16[16,72,128]{2,1,0:T(8,128)(2,1)S(1)} %pad_maximum_fusion.1), channel_id=1, source_target_pairs={{0,32},{8,40},{16,48},{24,56},{32,64},{40,72},{48,80},{56,88},{64,... | collective-permute-start | bytes 884744 | tf_op jit(solution)/shard_map/ppermute | solution.py:16
  29.1 5.8 %collective-permute-start.2 = (bf16[16,72,128]{2,1,0:T(8,128)(2,1)S(1)}, bf16[16,72,128]{2,1,0:T(8,128)(2,1)}, u32[]{:S(2)}, u32[]{:S(2)}) collective-permute-start(bf16[16,72,128]{2,1,0:T(8,128)(2,1)S(1)} %pad_maximum_fusion.1), channel_id=1, source_target_pairs={{0,24},{8,32},{16,40},{24,48},{32,56},{40,64},{48,72},{56,80},{64,... | collective-permute-start | bytes 884744 | tf_op jit(solution)/shard_map/ppermute | solution.py:16
  34.9 2.5 broadcast_in_dim.22
  37.4 5.4 %all-to-all-start.1 = ((bf16[256,8,512]{2,0,1:T(8,128)(2,1)}), bf16[256,8,512]{2,0,1:T(8,128)(2,1)S(1)}, u32[]{:S(2)}, u32[]{:S(2)}) async-start(bf16[256,8,512]{2,0,1:T(8,128)(2,1)} %broadcast_in_dim.22), calls=%async_computation.1 | async-start | bytes 4194304 | tf_op jit(solution)/shard_map/all_to_all | solution.py:61
  45.1 6.3 %collective-permute-done.2 = bf16[16,72,128]{2,1,0:T(8,128)(2,1)} collective-permute-done((bf16[16,72,128]{2,1,0:T(8,128)(2,1)S(1)}, bf16[16,72,128]{2,1,0:T(8,128)(2,1)}, u32[]{:S(2)}, u32[]{:S(2)}) %collective-permute-start.2) | collective-permute-done | bytes 294944 | tf_op jit(solution)/shard_map/ppermute | solution.py:16
  54.3 9.7 %collective-permute-start.5 = (bf16[16,72,128]{2,1,0:T(8,128)(2,1)S(1)}, bf16[16,72,128]{2,1,0:T(8,128)(2,1)S(1)}, u32[]{:S(2)}, u32[]{:S(2)}) collective-permute-start(bf16[16,72,128]{2,1,0:T(8,128)(2,1)S(1)} %pad_maximum_fusion.2), channel_id=1, source_target_pairs={{0,64},{8,72},{16,80},{24,88},{32,96},{40,104},{48,112},{56,120},{... | collective-permute-start | bytes 884744 | tf_op jit(solution)/shard_map/ppermute | solution.py:16
  64.0 3.0 %collective-permute-start.4 = (bf16[16,72,128]{2,1,0:T(8,128)(2,1)S(1)}, bf16[16,72,128]{2,1,0:T(8,128)(2,1)S(1)}, u32[]{:S(2)}, u32[]{:S(2)}) collective-permute-start(bf16[16,72,128]{2,1,0:T(8,128)(2,1)S(1)} %pad_maximum_fusion.2), channel_id=1, source_target_pairs={{0,32},{8,40},{16,48},{24,56},{32,64},{40,72},{48,80},{56,88},{64,... | collective-permute-start | bytes 884744 | tf_op jit(solution)/shard_map/ppermute | solution.py:16
  68.8 45.1 %collective-permute-done.5 = bf16[16,72,128]{2,1,0:T(8,128)(2,1)S(1)} collective-permute-done((bf16[16,72,128]{2,1,0:T(8,128)(2,1)S(1)}, bf16[16,72,128]{2,1,0:T(8,128)(2,1)S(1)}, u32[]{:S(2)}, u32[]{:S(2)}) %collective-permute-start.5) | collective-permute-done | bytes 294944 | tf_op jit(solution)/shard_map/ppermute | solution.py:16
  116.4 3.4 %fusion.27 = f32[256,16,64]{0,2,1:T(8,128)} fusion(bf16[256,16,64]{0,2,1:T(8,128)(2,1)S(1)} %bitcast.125, f32[16,256]{1,0:T(8,128)S(1)} %copy_bitcast_fusion.1, f32[256,256]{1,0:T(8,128)S(1)} %fusion.107, pred[256,256]{1,0:T(8,128)(4,1)S(1)} %fusion.61, f32[256,16,64]{0,2,1:T(8,128)S(1)} %convolution_bitcast_fusion.1, f32[256,16]{0,1:T(8,128)S(1)} %get-tuple-element.169), kind=kOutput, calls=%fused_computation.35 | convolution fusion | flops 407371776 | bytes 2981888 | tf_op jit(solution)/shard_map/jvp(hts,shp->thp)/dot_general | solution.py:95
  119.8 2.6 copy.72
  122.4 2.4 copy.74
  124.8 7.9 %multiply_reduce_fusion.1 = (f32[256]{0:T(256)S(1)}, f32[256]{0:T(256)S(1)}, f32[256,1024]{1,0:T(8,128)}) fusion(f32[256,1024]{1,0:T(8,128)} %copy.72, bf16[256,1024]{1,0:T(8,128)(2,1)S(1)} %copy-done.10, f32[1024]{0:T(1024)} %param.31, bf16[256,4096]{0,1:T(8,128)(2,1)} %bitcast.128, bf16[4096,1024]{1,0:T(8,128)(2,1)} %all-gather.2.cloned.1.call-done), kind=kOutput, calls=%fused_computation.56 | convolution fusion | flops 2150366720 | bytes 13113344 | tf_op jit(solution)/shard_map/dot_general | solution.py:178
  133.3 6.0 %convert_bitcast_fusion = bf16[4096,1024]{0,1:T(8,128)(2,1)} fusion(bf16[256,4096]{0,1:T(8,128)(2,1)S(1)} %bitcast.129, f32[1024]{0:T(1024)S(1)} %copy-done.33, f32[256]{0:T(256)S(1)} %get-tuple-element.174, f32[256,1024]{1,0:T(8,128)S(1)} %copy-done.6, bf16[256,1024]{1,0:T(8,128)(2,1)S(1)} %copy-done.10), kind=kOutput, calls=%fused_computation | convolution fusion | flops 2154037248 | bytes 12063744 | tf_op jit(solution)/shard_map/dot_general | solution.py:180
  139.3 6.0 %convolution_convert_fusion = bf16[256,4096]{1,0:T(8,128)(2,1)S(1)} fusion(bf16[4096,1024]{1,0:T(8,128)(2,1)} %all-gather.2.cloned.1.call-done, f32[1024]{0:T(1024)S(1)} %copy-done.33, f32[256]{0:T(256)S(1)} %get-tuple-element.174, f32[256,1024]{1,0:T(8,128)S(1)} %copy-done.6, bf16[256,1024]{1,0:T(8,128)(2,1)S(1)} %copy-done.10), kind=kOutput, calls=%fused_computation.4 | convolution fusion | flops 2150891520 | bytes 12063744 | tf_op jit(solution)/shard_map/dot_general | solution.py:173
  146.8 5.4 %all-to-all-start = ((bf16[256,8,512]{2,0,1:T(8,128)(2,1)}), bf16[256,8,512]{2,0,1:T(8,128)(2,1)S(1)}, u32[]{:S(2)}, u32[]{:S(2)}) async-start(bf16[256,8,512]{2,0,1:T(8,128)(2,1)} %bitcast.123), calls=%async_computation | async-start | bytes 4194304 | tf_op jit(solution)/shard_map/all_to_all | solution.py:69
  152.2 3.6 %fusion.44 = (f32[256,1024]{1,0:T(8,128)}, f32[256,1024]{1,0:T(8,128)}) fusion(bf16[256,1024]{1,0:T(8,128)(2,1)} %param.28, f32[256,1024]{1,0:T(8,128)S(1)} %copy-done.6, f32[256]{0:T(256)} %get-tuple-element.173, f32[256,1024]{1,0:T(8,128)} %get-tuple-element.179, f32[256]{0:T(256)} %copy-done.31), kind=kLoop, calls=%fused_computation.52 | loop fusion | flops 4718592 | bytes 4720640 | tf_op jit(solution)/shard_map/transpose(jvp(jit(silu)))/add_any | solution.py:109
  161.6 5.6 %fusion.54 = (f32[16,256]{1,0:T(8,128)S(1)}, f32[16,256]{1,0:T(8,128)S(1)}, f32[256,256]{1,0:T(8,128)S(1)}) fusion(f32[16,256]{1,0:T(8,128)} %copy-done.19, f32[256,256]{1,0:T(8,128)} %copy-done.12, pred[256,256]{1,0:T(8,128)(4,1)} %copy-done.18, f32[16,64,256]{2,1,0:T(8,128)S(1)} %bitcast.120, bf16[256,16,64]{0,2,1:T(8,128)(2,1)} %bitcast.126), kind=kOutput, calls=%fused_computation.66 | convolution fusion | flops 418308096 | bytes 2211840 | tf_op jit(solution)/shard_map/transpose(jvp(hts,shp->thp))/dot_general | solution.py:95
  173.4 2.5 reduce-window.41
  177.0 13.4 %collective-permute-done.8 = bf16[16,72,128]{2,1,0:T(8,128)(2,1)} collective-permute-done((bf16[16,72,128]{2,1,0:T(8,128)(2,1)}, bf16[16,72,128]{2,1,0:T(8,128)(2,1)}, u32[]{:S(2)}, u32[]{:S(2)}) %collective-permute-start.8) | collective-permute-done | bytes 294944 | tf_op jit(solution)/shard_map/ppermute | solution.py:16
  192.8 2.3 fusion.93
  201.7 27.0 %collective-permute-done.12 = bf16[16,72,128]{2,1,0:T(8,128)(2,1)} collective-permute-done((bf16[16,72,128]{2,1,0:T(8,128)(2,1)}, bf16[16,72,128]{2,1,0:T(8,128)(2,1)}, u32[]{:S(2)}, u32[]{:S(2)}) %collective-permute-start.12) | collective-permute-done | bytes 294944 | tf_op jit(solution)/shard_map/ppermute | solution.py:16
  229.7 4.8 %collective-permute-done.13 = bf16[16,72,128]{2,1,0:T(8,128)(2,1)S(1)} collective-permute-done((bf16[16,72,128]{2,1,0:T(8,128)(2,1)}, bf16[16,72,128]{2,1,0:T(8,128)(2,1)S(1)}, u32[]{:S(2)}, u32[]{:S(2)}) %collective-permute-start.13) | collective-permute-done | bytes 294944 | tf_op jit(solution)/shard_map/ppermute | solution.py:16
  234.5 2.2 multiply_reduce_fusion.3
  238.1 4.0 %fusion.30 = f32[256,16,64]{0,2,1:T(8,128)} fusion(f32[16,64,256]{2,1,0:T(8,128)S(1)} %bitcast.122, f32[16,256]{1,0:T(8,128)S(1)} %copy-done.20, f32[256,256]{1,0:T(8,128)S(1)} %copy-done.13, pred[256,256]{1,0:T(8,128)(4,1)} %copy-done.18, f32[256,16,64]{0,2,1:T(8,128)S(1)} %get-tuple-element.181, f32[256,16]{0,1:T(8,128)S(1)} %copy-done.17), kind=kOutput, calls=%fused_computation.36 | convolution fusion | flops 407371776 | bytes 3506176 | tf_op jit(solution)/shard_map/transpose(jvp(hts,shp->thp))/dot_general | solution.py:95
  242.2 2.7 copy.82
  245.2 2.5 reduce-window.49
  247.9 2.5 reduce-window.45
  251.2 2.9 %fusion.38 = f32[256,128]{1,0:T(8,128)} fusion(f32[256,128]{1,0:T(8,128)S(1)} %fusion.108, f32[16,64,128]{2,1,0:T(8,128)} %copy-done.4, bf16[256,16,64]{0,2,1:T(8,128)(2,1)} %bitcast.127, f32[256,16]{0,1:T(8,128)S(1)} %copy-done.17), kind=kOutput, calls=%fused_computation.46 | convolution fusion | flops 201883648 | bytes 1327104 | tf_op jit(solution)/shard_map/transpose(jvp(shp,shn->hpn))/dot_general | solution.py:103
  255.1 6.1 %reduce-scatter.2.cloned.1.call-done = bf16[256,1024]{0,1:T(8,128)(2,1)} async-done(((bf16[4096,1024]{0,1:T(8,128)(2,1)}), bf16[256,1024]{0,1:T(8,128)(2,1)}) %reduce-scatter.2.cloned.1.call-update) | async-done | bytes 524304 | tf_op jit(solution)/shard_map/reduce_scatter | solution.py:179
  261.2 2.2 copy.83
  (171 shorter events, 48.2 us)
Async XLA Ops:
  7.2 117.6 %all-gather.2.cloned.1.call-start = ((), (), s32[]{:S(2)}) async-start(), calls=%async_computation.3 | async-start | bytes 8912896 | tf_op jit(solution)/shard_map/all_gather | solution.py:172
  16.2 100.2 %copy-start = (bf16[256,1024]{0,1:T(8,128)(2,1)}, bf16[256,1024]{0,1:T(8,128)(2,1)S(1)}, u32[]{:S(2)}) copy-start(bf16[256,1024]{0,1:T(8,128)(2,1)S(1)} %copy.71) | copy-start | bytes 1572868
  16.5 36.3 %copy-start.11 = (bf16[16,8,128]{2,1,0:T(8,128)(2,1)}, bf16[16,8,128]{2,1,0:T(8,128)(2,1)S(1)}, u32[]{:S(2)}) copy-start(bf16[16,8,128]{2,1,0:T(8,128)(2,1)S(1)} %scatter.21) | copy-start | bytes 98308
  16.5 99.8 %copy-start.19 = (f32[16,256]{1,0:T(8,128)}, f32[16,256]{1,0:T(8,128)S(1)}, u32[]{:S(2)}) copy-start(f32[16,256]{1,0:T(8,128)S(1)} %copy_bitcast_fusion.1) | copy-start | bytes 49156
  16.7 34.7 %copy-start.27 = (f32[16]{0:T(128)}, f32[16]{0:T(128)S(1)}, u32[]{:S(2)}) copy-start(f32[16]{0:T(128)S(1)} %slice_reduce_fusion.4) | copy-start | bytes 196
  17.5 36.8 %copy-start.16 = (f32[256,16]{0,1:T(8,128)}, f32[256,16]{0,1:T(8,128)S(1)}, u32[]{:S(2)}) copy-start(f32[256,16]{0,1:T(8,128)S(1)} %get-tuple-element.170) | copy-start | bytes 49156
  17.5 98.9 %copy-start.14 = (f32[256,16]{0,1:T(8,128)}, f32[256,16]{0,1:T(8,128)S(1)}, u32[]{:S(2)}) copy-start(f32[256,16]{0,1:T(8,128)S(1)} %get-tuple-element.169) | copy-start | bytes 49156
  18.1 48.8 %copy-start.8 = (bf16[256,128]{1,0:T(8,128)(2,1)S(1)}, bf16[256,128]{1,0:T(8,128)(2,1)}, u32[]{:S(2)}) copy-start(bf16[256,128]{1,0:T(8,128)(2,1)} %param.26) | copy-start | bytes 196612
  18.1 48.8 %copy-start.9 = (bf16[256,128]{1,0:T(8,128)(2,1)S(1)}, bf16[256,128]{1,0:T(8,128)(2,1)}, u32[]{:S(2)}) copy-start(bf16[256,128]{1,0:T(8,128)(2,1)} %param.27) | copy-start | bytes 196612
  18.2 24.7 %collective-permute-start = (bf16[16,72,128]{2,1,0:T(8,128)(2,1)S(1)}, bf16[16,72,128]{2,1,0:T(8,128)(2,1)}, u32[]{:S(2)}, u32[]{:S(2)}) collective-permute-start(bf16[16,72,128]{2,1,0:T(8,128)(2,1)S(1)} %pad_maximum_fusion.1), channel_id=1, source_target_pairs={{0,8},{8,16},{16,24},{24,32},{32,40},{40,48},{48,56},{56,64},{64,7... | collective-permute-start | bytes 884744 | tf_op jit(solution)/shard_map/ppermute | solution.py:16
  20.3 23.6 %collective-permute-start.1 = (bf16[16,72,128]{2,1,0:T(8,128)(2,1)S(1)}, bf16[16,72,128]{2,1,0:T(8,128)(2,1)}, u32[]{:S(2)}, u32[]{:S(2)}) collective-permute-start(bf16[16,72,128]{2,1,0:T(8,128)(2,1)S(1)} %pad_maximum_fusion.1), channel_id=1, source_target_pairs={{0,16},{8,24},{16,32},{24,40},{32,48},{40,56},{48,64},{56,72},{64,... | collective-permute-start | bytes 884744 | tf_op jit(solution)/shard_map/ppermute | solution.py:16
  24.4 20.6 %collective-permute-start.3 = (bf16[16,72,128]{2,1,0:T(8,128)(2,1)S(1)}, bf16[16,72,128]{2,1,0:T(8,128)(2,1)}, u32[]{:S(2)}, u32[]{:S(2)}) collective-permute-start(bf16[16,72,128]{2,1,0:T(8,128)(2,1)S(1)} %pad_maximum_fusion.1), channel_id=1, source_target_pairs={{0,32},{8,40},{16,48},{24,56},{32,64},{40,72},{48,80},{56,88},{64,... | collective-permute-start | bytes 884744 | tf_op jit(solution)/shard_map/ppermute | solution.py:16
  29.1 22.3 %collective-permute-start.2 = (bf16[16,72,128]{2,1,0:T(8,128)(2,1)S(1)}, bf16[16,72,128]{2,1,0:T(8,128)(2,1)}, u32[]{:S(2)}, u32[]{:S(2)}) collective-permute-start(bf16[16,72,128]{2,1,0:T(8,128)(2,1)S(1)} %pad_maximum_fusion.1), channel_id=1, source_target_pairs={{0,24},{8,32},{16,40},{24,48},{32,56},{40,64},{48,72},{56,80},{64,... | collective-permute-start | bytes 884744 | tf_op jit(solution)/shard_map/ppermute | solution.py:16
  37.4 85.0 %all-to-all-start.1 = ((bf16[256,8,512]{2,0,1:T(8,128)(2,1)}), bf16[256,8,512]{2,0,1:T(8,128)(2,1)S(1)}, u32[]{:S(2)}, u32[]{:S(2)}) async-start(bf16[256,8,512]{2,0,1:T(8,128)(2,1)} %broadcast_in_dim.22), calls=%async_computation.1 | async-start | bytes 4194304 | tf_op jit(solution)/shard_map/all_to_all | solution.py:61
  42.8 218.4 %reduce-scatter.2.cloned.1.call-start = ((), (), s32[]{:S(2)}) async-start(), calls=%async_computation.4 | async-start | bytes 8912896 | tf_op jit(solution)/shard_map/reduce_scatter | solution.py:179
  54.3 59.6 %collective-permute-start.5 = (bf16[16,72,128]{2,1,0:T(8,128)(2,1)S(1)}, bf16[16,72,128]{2,1,0:T(8,128)(2,1)S(1)}, u32[]{:S(2)}, u32[]{:S(2)}) collective-permute-start(bf16[16,72,128]{2,1,0:T(8,128)(2,1)S(1)} %pad_maximum_fusion.2), channel_id=1, source_target_pairs={{0,64},{8,72},{16,80},{24,88},{32,96},{40,104},{48,112},{56,120},{... | collective-permute-start | bytes 884744 | tf_op jit(solution)/shard_map/ppermute | solution.py:16
  64.0 49.9 %collective-permute-start.4 = (bf16[16,72,128]{2,1,0:T(8,128)(2,1)S(1)}, bf16[16,72,128]{2,1,0:T(8,128)(2,1)S(1)}, u32[]{:S(2)}, u32[]{:S(2)}) collective-permute-start(bf16[16,72,128]{2,1,0:T(8,128)(2,1)S(1)} %pad_maximum_fusion.2), channel_id=1, source_target_pairs={{0,32},{8,40},{16,48},{24,56},{32,64},{40,72},{48,80},{56,88},{64,... | collective-permute-start | bytes 884744 | tf_op jit(solution)/shard_map/ppermute | solution.py:16
  67.2 52.6 %copy-start.12 = (f32[256,256]{1,0:T(8,128)}, f32[256,256]{1,0:T(8,128)S(1)}, u32[]{:S(2)}) copy-start(f32[256,256]{1,0:T(8,128)S(1)} %fusion.107) | copy-start | bytes 786436
  67.2 46.9 %collective-permute-start.6 = (bf16[16,72,128]{2,1,0:T(8,128)(2,1)S(1)}, bf16[16,72,128]{2,1,0:T(8,128)(2,1)S(1)}, u32[]{:S(2)}, u32[]{:S(2)}) collective-permute-start(bf16[16,72,128]{2,1,0:T(8,128)(2,1)S(1)} %pad_maximum_fusion.2), channel_id=1, source_target_pairs={{0,96},{8,104},{16,112},{24,120},{1,97},{9,105},{17,113},{25,121},... | collective-permute-start | bytes 884744 | tf_op jit(solution)/shard_map/ppermute | solution.py:16
  68.8 51.0 %copy-start.18 = (pred[256,256]{1,0:T(8,128)(4,1)}, pred[256,256]{1,0:T(8,128)(4,1)S(1)}, u32[]{:S(2)}) copy-start(pred[256,256]{1,0:T(8,128)(4,1)S(1)} %fusion.61) | copy-start | bytes 196612
  146.8 107.3 %all-to-all-start = ((bf16[256,8,512]{2,0,1:T(8,128)(2,1)}), bf16[256,8,512]{2,0,1:T(8,128)(2,1)S(1)}, u32[]{:S(2)}, u32[]{:S(2)}) async-start(bf16[256,8,512]{2,0,1:T(8,128)(2,1)} %bitcast.123), calls=%async_computation | async-start | bytes 4194304 | tf_op jit(solution)/shard_map/all_to_all | solution.py:69
  160.3 15.6 %collective-permute-start.7 = (bf16[16,72,128]{2,1,0:T(8,128)(2,1)}, bf16[16,72,128]{2,1,0:T(8,128)(2,1)}, u32[]{:S(2)}, u32[]{:S(2)}) collective-permute-start(bf16[16,72,128]{2,1,0:T(8,128)(2,1)} %pad_maximum_fusion), channel_id=1, source_target_pairs={{8,0},{16,8},{24,16},{32,24},{40,32},{48,40},{56,48},{64,56},{72,6... | collective-permute-start | bytes 884744 | tf_op jit(solution)/shard_map/ppermute | solution.py:16
  169.5 21.9 %collective-permute-start.10 = (bf16[16,72,128]{2,1,0:T(8,128)(2,1)}, bf16[16,72,128]{2,1,0:T(8,128)(2,1)}, u32[]{:S(2)}, u32[]{:S(2)}) collective-permute-start(bf16[16,72,128]{2,1,0:T(8,128)(2,1)} %pad_maximum_fusion), channel_id=1, source_target_pairs={{32,0},{40,8},{48,16},{56,24},{64,32},{72,40},{80,48},{88,56},{96,... | collective-permute-start | bytes 884744 | tf_op jit(solution)/shard_map/ppermute | solution.py:16
  170.8 20.6 %collective-permute-start.9 = (bf16[16,72,128]{2,1,0:T(8,128)(2,1)}, bf16[16,72,128]{2,1,0:T(8,128)(2,1)}, u32[]{:S(2)}, u32[]{:S(2)}) collective-permute-start(bf16[16,72,128]{2,1,0:T(8,128)(2,1)} %pad_maximum_fusion), channel_id=1, source_target_pairs={{24,0},{32,8},{40,16},{48,24},{56,32},{64,40},{72,48},{80,56},{88,... | collective-permute-start | bytes 884744 | tf_op jit(solution)/shard_map/ppermute | solution.py:16
  172.1 18.3 %collective-permute-start.8 = (bf16[16,72,128]{2,1,0:T(8,128)(2,1)}, bf16[16,72,128]{2,1,0:T(8,128)(2,1)}, u32[]{:S(2)}, u32[]{:S(2)}) collective-permute-start(bf16[16,72,128]{2,1,0:T(8,128)(2,1)} %pad_maximum_fusion), channel_id=1, source_target_pairs={{16,0},{24,8},{32,16},{40,24},{48,32},{56,40},{64,48},{72,56},{80,... | collective-permute-start | bytes 884744 | tf_op jit(solution)/shard_map/ppermute | solution.py:16
  192.8 45.2 %copy-start.17 = (f32[256,16]{0,1:T(8,128)S(1)}, f32[256,16]{0,1:T(8,128)}, u32[]{:S(2)}) copy-start(f32[256,16]{0,1:T(8,128)} %copy-done.16) | copy-start | bytes 49156
  192.8 45.2 %copy-start.20 = (f32[16,256]{1,0:T(8,128)S(1)}, f32[16,256]{1,0:T(8,128)}, u32[]{:S(2)}) copy-start(f32[16,256]{1,0:T(8,128)} %copy-done.19) | copy-start | bytes 49156
  195.9 32.8 %collective-permute-start.12 = (bf16[16,72,128]{2,1,0:T(8,128)(2,1)}, bf16[16,72,128]{2,1,0:T(8,128)(2,1)}, u32[]{:S(2)}, u32[]{:S(2)}) collective-permute-start(bf16[16,72,128]{2,1,0:T(8,128)(2,1)} %pad_maximum_fusion.3), channel_id=1, source_target_pairs={{64,0},{72,8},{80,16},{88,24},{96,32},{104,40},{112,48},{120,56},{... | collective-permute-start | bytes 884744 | tf_op jit(solution)/shard_map/ppermute | solution.py:16
  197.2 31.5 %collective-permute-start.11 = (bf16[16,72,128]{2,1,0:T(8,128)(2,1)}, bf16[16,72,128]{2,1,0:T(8,128)(2,1)}, u32[]{:S(2)}, u32[]{:S(2)}) collective-permute-start(bf16[16,72,128]{2,1,0:T(8,128)(2,1)} %pad_maximum_fusion.3), channel_id=1, source_target_pairs={{32,0},{40,8},{48,16},{56,24},{64,32},{72,40},{80,48},{88,56},{96,... | collective-permute-start | bytes 884744 | tf_op jit(solution)/shard_map/ppermute | solution.py:16
  198.6 38.2 %copy-start.1 = (bf16[256,1024]{0,1:T(8,128)(2,1)S(1)}, bf16[256,1024]{0,1:T(8,128)(2,1)}, u32[]{:S(2)}) copy-start(bf16[256,1024]{0,1:T(8,128)(2,1)} %copy-done) | copy-start | bytes 1572868
  198.6 39.5 %copy-start.13 = (f32[256,256]{1,0:T(8,128)S(1)}, f32[256,256]{1,0:T(8,128)}, u32[]{:S(2)}) copy-start(f32[256,256]{1,0:T(8,128)} %copy-done.12) | copy-start | bytes 786436
  198.6 35.9 %collective-permute-start.13 = (bf16[16,72,128]{2,1,0:T(8,128)(2,1)}, bf16[16,72,128]{2,1,0:T(8,128)(2,1)S(1)}, u32[]{:S(2)}, u32[]{:S(2)}) collective-permute-start(bf16[16,72,128]{2,1,0:T(8,128)(2,1)} %pad_maximum_fusion.3), channel_id=1, source_target_pairs={{96,0},{104,8},{112,16},{120,24},{97,1},{105,9},{113,17},{121,25},... | collective-permute-start | bytes 884744 | tf_op jit(solution)/shard_map/ppermute | solution.py:16
  (20 other events, 206.8 us)
Sparse Core Ops, SparseCore 0:
  10.4 97.3 all-gather.1
  139.4 121.7 reduce-scatter.1

commit v2 on v1

--- a/solution.py
+++ b/solution.py
@@ -176,14 +176,18 @@
     layer_out = head_sum_scatter(partial_value.astype(jnp.bfloat16)).astype(jnp.bfloat16)
     grad_full = head_gather(out_grad)
     grad_y = jnp.dot(grad_full, full_weight, preferred_element_type=jnp.float32)
-    grad_weight = lax.psum_scatter(
-        lax.dot_general(
-            grad_full, normed_bf, (((0,), (0,)), ((), ())), preferred_element_type=jnp.float32
-        ).astype(jnp.bfloat16),
+    seq_count = lax.axis_size("seq")
+    weight_term = lax.dot_general(
+        grad_full, normed_bf, (((0,), (0,)), ((), ())), preferred_element_type=jnp.float32
+    ).astype(jnp.bfloat16)
+    weight_blocks = lax.all_to_all(
+        weight_term.reshape(seq_count, -1, weight_term.shape[1]),
         "seq",
-        scatter_dimension=0,
+        split_axis=0,
+        concat_axis=0,
         tiled=True,
-    ).astype(jnp.float32)
+    )
+    grad_weight = jnp.sum(weight_blocks.astype(jnp.float32), axis=0)
     d_zero, d_c_two, d_decay_two, grad_z, adjoint_in = pull_finish(grad_y)
 
     adjoint_out = prefix_combine(g_local, adjoint_in, -1)

time: 272 us -> 373 us (1.37)
  waiting for transfers between devices: 104 us -> 187 us
  starting transfers between devices: 51.2 us -> 57.3 us
  other arithmetic: 37 us -> 42.3 us
  local copies, waits for them, and re-layouts: 20.6 us -> 25.9 us
    ppermute x14, waiting for transfers between devices: 96.8 us -> 174 us  [from_behind(): lax.ppermute(value, axis, [(source, source + steps) for source in range(l...]
    all_to_all x1, waiting for transfers between devices: 0.01 us -> 12.1 us  [head_sum_scatter(): lax.all_to_all(pieces, 'head', split_axis=1, concat_axis=1, tiled=True)]
    reshape x0 -> x1, local copies, waits for them, and re-layouts: none -> 7.44 us  [per_device(): weight_term.reshape(seq_count, -1, weight_term.shape[1])]
    reduce_scatter x1 -> x0, waiting for transfers between devices: 6.1 us -> none  [per_device(): lax.psum_scatter(lax.dot_general(grad_full, normed_bf, (((0,), (0,)), (()...]
    all_to_all x0 -> x1, starting transfers between devices: none -> 6.02 us  [per_device(): lax.all_to_all(weight_term.reshape(seq_count, -1, weight_term.shape[1]),...]
    reduce_sum x0 -> x1, other arithmetic: none -> 4.65 us  [per_device(): grad_weight = jnp.sum(weight_blocks.astype(jnp.float32), axis=0)]
  transfers between devices with their start and end apart: 18 -> 18, of which waited for: 7 -> 7; matrix products, arithmetic and copies ran while one was open for 31% -> 24% of each run, Pallas kernels for 0% -> 0%
where the time goes in v2:
time: 373 us; the launch traced here: 368 us
  waiting for transfers between devices  187 us (50%)
  starting transfers between devices  57.3 us (15%)
  other arithmetic  42.3 us (11%)
  matrix products  40.7 us (11%)
  local copies, waits for them, and re-layouts  25.9 us (7%)
  between operations  15.4 us (4%)
    ppermute x14, waiting for transfers between devices, from_behind(): lax.ppermute(value, axis, [(source, source + steps) for source in range(l...  174 us
    ppermute x14, starting transfers between devices, from_behind(): lax.ppermute(value, axis, [(source, source + steps) for source in range(l...  40.5 us
    dot_general x3, matrix products, block_outputs(): jnp.einsum('hts,shp->thp', scores, x_heads, precision=lax.Precision.HIGH)  13 us
    all_to_all x1, waiting for transfers between devices, head_sum_scatter(): lax.all_to_all(pieces, 'head', split_axis=1, concat_axis=1, tiled=True)  12.1 us
    another operation x11, other arithmetic  9.3 us
    dot_general x1, matrix products, per_device(): lax.dot_general(grad_full, normed_bf, (((0,), (0,)), ((), ())), preferred...  7.72 us
    dot_general x1, matrix products, per_device(): grad_y = jnp.dot(grad_full, full_weight, preferred_element_type=jnp.float32)  7.72 us
  transfers between devices with their start and end apart: 18, of which 7 were waited for; matrix products, arithmetic and copies ran while one was open for 24% of the time, Pallas kernels for 0%

profile of v2, /device:TPU:0, one launch (start us, length us, event | category | flops | bytes accessed | tf_op | source)
XLA Modules:
  0.0 368.0 jit_solution(11559329876826623194)
XLA Ops:
  21.0 4.2 %collective-permute-start.1 = (bf16[16,72,128]{2,1,0:T(8,128)(2,1)}, bf16[16,72,128]{2,1,0:T(8,128)(2,1)}, u32[]{:S(2)}, u32[]{:S(2)}) collective-permute-start(bf16[16,72,128]{2,1,0:T(8,128)(2,1)} %pad_maximum_fusion.1), channel_id=1, source_target_pairs={{0,16},{8,24},{16,32},{24,40},{32,48},{40,56},{48,64},{56,72},{64,... | collective-permute-start | bytes 884744 | tf_op jit(solution)/shard_map/ppermute | solution.py:16
  25.1 4.7 %collective-permute-start.3 = (bf16[16,72,128]{2,1,0:T(8,128)(2,1)}, bf16[16,72,128]{2,1,0:T(8,128)(2,1)}, u32[]{:S(2)}, u32[]{:S(2)}) collective-permute-start(bf16[16,72,128]{2,1,0:T(8,128)(2,1)} %pad_maximum_fusion.1), channel_id=1, source_target_pairs={{0,32},{8,40},{16,48},{24,56},{32,64},{40,72},{48,80},{56,88},{64,... | collective-permute-start | bytes 884744 | tf_op jit(solution)/shard_map/ppermute | solution.py:16
  29.8 5.8 %collective-permute-start.2 = (bf16[16,72,128]{2,1,0:T(8,128)(2,1)}, bf16[16,72,128]{2,1,0:T(8,128)(2,1)}, u32[]{:S(2)}, u32[]{:S(2)}) collective-permute-start(bf16[16,72,128]{2,1,0:T(8,128)(2,1)} %pad_maximum_fusion.1), channel_id=1, source_target_pairs={{0,24},{8,32},{16,40},{24,48},{32,56},{40,64},{48,72},{56,80},{64,... | collective-permute-start | bytes 884744 | tf_op jit(solution)/shard_map/ppermute | solution.py:16
  35.6 2.5 broadcast_in_dim.22
  38.1 5.4 %all-to-all-start.1 = ((bf16[256,8,512]{2,0,1:T(8,128)(2,1)}), bf16[256,8,512]{2,0,1:T(8,128)(2,1)S(1)}, u32[]{:S(2)}, u32[]{:S(2)}) async-start(bf16[256,8,512]{2,0,1:T(8,128)(2,1)} %broadcast_in_dim.22), calls=%async_computation.1 | async-start | bytes 4194304 | tf_op jit(solution)/shard_map/all_to_all | solution.py:61
  45.6 6.2 %collective-permute-done.2 = bf16[16,72,128]{2,1,0:T(8,128)(2,1)} collective-permute-done((bf16[16,72,128]{2,1,0:T(8,128)(2,1)}, bf16[16,72,128]{2,1,0:T(8,128)(2,1)}, u32[]{:S(2)}, u32[]{:S(2)}) %collective-permute-start.2) | collective-permute-done | bytes 294944 | tf_op jit(solution)/shard_map/ppermute | solution.py:16
  54.7 10.1 %collective-permute-start.5 = (bf16[16,72,128]{2,1,0:T(8,128)(2,1)S(1)}, bf16[16,72,128]{2,1,0:T(8,128)(2,1)S(1)}, u32[]{:S(2)}, u32[]{:S(2)}) collective-permute-start(bf16[16,72,128]{2,1,0:T(8,128)(2,1)S(1)} %pad_maximum_fusion.2), channel_id=1, source_target_pairs={{0,64},{8,72},{16,80},{24,88},{32,96},{40,104},{48,112},{56,120},{... | collective-permute-start | bytes 884744 | tf_op jit(solution)/shard_map/ppermute | solution.py:16
  64.8 2.9 collective-permute-start.4
  69.5 44.6 %collective-permute-done.5 = bf16[16,72,128]{2,1,0:T(8,128)(2,1)S(1)} collective-permute-done((bf16[16,72,128]{2,1,0:T(8,128)(2,1)S(1)}, bf16[16,72,128]{2,1,0:T(8,128)(2,1)S(1)}, u32[]{:S(2)}, u32[]{:S(2)}) %collective-permute-start.5) | collective-permute-done | bytes 294944 | tf_op jit(solution)/shard_map/ppermute | solution.py:16
  116.6 3.4 fusion.27
  121.6 2.4 copy.73
  124.0 7.7 %multiply_reduce_fusion.1 = (f32[256]{0:T(256)S(1)}, f32[256]{0:T(256)S(1)}, f32[256,1024]{1,0:T(8,128)}) fusion(f32[256,1024]{1,0:T(8,128)S(1)} %copy.71, bf16[256,1024]{1,0:T(8,128)(2,1)} %param.28, f32[1024]{0:T(1024)} %param.31, bf16[256,4096]{0,1:T(8,128)(2,1)} %bitcast.133, bf16[4096,1024]{1,0:T(8,128)(2,1)} %all-gather.2.cloned.1.call-done), kind=kOutput, calls=%fused_computation.58 | convolution fusion | flops 2150366720 | bytes 13113344 | tf_op jit(solution)/shard_map/dot_general | solution.py:178
  132.3 2.7 convolution_convert_fusion.1
  136.4 5.3 %all-to-all-start = ((bf16[256,8,512]{2,0,1:T(8,128)(2,1)}), bf16[256,8,512]{2,0,1:T(8,128)(2,1)S(1)}, u32[]{:S(2)}, u32[]{:S(2)}) async-start(bf16[256,8,512]{2,0,1:T(8,128)(2,1)} %bitcast.128), calls=%async_computation | async-start | bytes 4194304 | tf_op jit(solution)/shard_map/all_to_all | solution.py:69
  141.8 7.7 %convolution_convert_fusion = bf16[1024,4096]{1,0:T(8,128)(2,1)} fusion(bf16[256,4096]{0,1:T(8,128)(2,1)} %bitcast.134, f32[1024]{0:T(1024)} %param.31, f32[256]{0:T(256)} %copy-done.29, f32[256,1024]{1,0:T(8,128)S(1)} %copy.71, bf16[256,1024]{1,0:T(8,128)(2,1)} %param.28), kind=kOutput, calls=%fused_computation.5 | convolution fusion | flops 2154037248 | bytes 12063744 | tf_op jit(solution)/shard_map/dot_general | solution.py:180
  149.5 7.4 %copy.112 = bf16[128,16,8,256]{3,2,0,1:T(8,128)(2,1)} copy(bf16[128,16,8,256]{3,2,1,0:T(8,128)(2,1)} %bitcast.127) | data formatting | bytes 16777216 | tf_op jit(solution)/shard_map/reshape | solution.py:184
  156.9 12.1 %all-to-all-done = bf16[256,8,512]{2,0,1:T(8,128)(2,1)S(1)} async-done(((bf16[256,8,512]{2,0,1:T(8,128)(2,1)}), bf16[256,8,512]{2,0,1:T(8,128)(2,1)S(1)}, u32[]{:S(2)}, u32[]{:S(2)}) %all-to-all-start) | async-done | bytes 2097184 | tf_op jit(solution)/shard_map/all_to_all | solution.py:69
  169.0 6.0 %all-to-all-start.2 = ((bf16[16,256,1024]{1,2,0:T(8,128)(2,1)}), bf16[16,256,1024]{1,2,0:T(8,128)(2,1)}, u32[]{:S(2)}, u32[]{:S(2)}) async-start(bf16[16,256,1024]{1,2,0:T(8,128)(2,1)} %bitcast.122), calls=%async_computation.2 | async-start | bytes 16777216 | tf_op jit(solution)/shard_map/all_to_all | solution.py:183
  175.1 3.5 fusion.44
  184.2 5.5 %fusion.54 = (f32[16,256]{1,0:T(8,128)S(1)}, f32[16,256]{1,0:T(8,128)S(1)}, f32[256,256]{1,0:T(8,128)S(1)}) fusion(f32[16,256]{1,0:T(8,128)} %copy-done.17, f32[256,256]{1,0:T(8,128)} %copy-done.10, pred[256,256]{1,0:T(8,128)(4,1)} %copy-done.16, f32[16,64,256]{2,1,0:T(8,128)S(1)} %bitcast.124, bf16[256,16,64]{0,2,1:T(8,128)(2,1)} %bitcast.131), kind=kOutput, calls=%fused_computation.68 | convolution fusion | flops 418308096 | bytes 2211840 | tf_op jit(solution)/shard_map/transpose(jvp(hts,shp->thp))/dot_general | solution.py:95
  195.9 2.5 reduce-window.41
  199.4 83.1 %collective-permute-done.8 = bf16[16,72,128]{2,1,0:T(8,128)(2,1)} collective-permute-done((bf16[16,72,128]{2,1,0:T(8,128)(2,1)}, bf16[16,72,128]{2,1,0:T(8,128)(2,1)}, u32[]{:S(2)}, u32[]{:S(2)}) %collective-permute-start.8) | collective-permute-done | bytes 294944 | tf_op jit(solution)/shard_map/ppermute | solution.py:16
  284.9 2.3 fusion.93
  293.7 16.9 %collective-permute-done.12 = bf16[16,72,128]{2,1,0:T(8,128)(2,1)} collective-permute-done((bf16[16,72,128]{2,1,0:T(8,128)(2,1)}, bf16[16,72,128]{2,1,0:T(8,128)(2,1)}, u32[]{:S(2)}, u32[]{:S(2)}) %collective-permute-start.12) | collective-permute-done | bytes 294944 | tf_op jit(solution)/shard_map/ppermute | solution.py:16
  310.6 15.1 %collective-permute-done.11 = bf16[16,72,128]{2,1,0:T(8,128)(2,1)} collective-permute-done((bf16[16,72,128]{2,1,0:T(8,128)(2,1)}, bf16[16,72,128]{2,1,0:T(8,128)(2,1)}, u32[]{:S(2)}, u32[]{:S(2)}) %collective-permute-start.11) | collective-permute-done | bytes 294944 | tf_op jit(solution)/shard_map/ppermute | solution.py:16
  326.9 7.9 %collective-permute-done.13 = bf16[16,72,128]{2,1,0:T(8,128)(2,1)S(1)} collective-permute-done((bf16[16,72,128]{2,1,0:T(8,128)(2,1)}, bf16[16,72,128]{2,1,0:T(8,128)(2,1)S(1)}, u32[]{:S(2)}, u32[]{:S(2)}) %collective-permute-start.13) | collective-permute-done | bytes 294944 | tf_op jit(solution)/shard_map/ppermute | solution.py:16
  338.4 4.0 %fusion.30 = f32[256,16,64]{0,2,1:T(8,128)} fusion(f32[16,64,256]{2,1,0:T(8,128)S(1)} %bitcast.126, f32[16,256]{1,0:T(8,128)S(1)} %copy-done.18, f32[256,256]{1,0:T(8,128)S(1)} %copy-done.11, pred[256,256]{1,0:T(8,128)(4,1)} %copy-done.16, f32[256,16,64]{0,2,1:T(8,128)S(1)} %get-tuple-element.181, f32[256,16]{0,1:T(8,128)S(1)} %copy-done.15), kind=kOutput, calls=%fused_computation.38 | convolution fusion | flops 407371776 | bytes 3506176 | tf_op jit(solution)/shard_map/transpose(jvp(hts,shp->thp))/dot_general | solution.py:95
  342.4 2.5 copy.83
  345.3 2.5 reduce-window.49
  348.0 2.5 reduce-window.45
  351.3 2.9 fusion.38
  355.2 4.6 %convert_reduce_fusion = f32[256,1024]{0,1:T(8,128)S(1)} fusion(bf16[16,256,1024]{1,2,0:T(8,128)(2,1)} %all-to-all-done.2), kind=kLoop, calls=%fused_computation | loop fusion | flops 8126464 | bytes 9437184 | tf_op jit(solution)/shard_map/reduce_sum | solution.py:190
  (170 shorter events, 55.6 us)
Async XLA Ops:
  7.2 116.8 %all-gather.2.cloned.1.call-start = ((), (), s32[]{:S(2)}) async-start(), calls=%async_computation.3 | async-start | bytes 8912896 | tf_op jit(solution)/shard_map/all_gather | solution.py:172
  16.2 100.4 %copy-start = (bf16[256,1024]{0,1:T(8,128)(2,1)}, bf16[256,1024]{0,1:T(8,128)(2,1)S(1)}, u32[]{:S(2)}) copy-start(bf16[256,1024]{0,1:T(8,128)(2,1)S(1)} %copy.70) | copy-start | bytes 1572868
  16.5 36.7 %copy-start.9 = (bf16[16,8,128]{2,1,0:T(8,128)(2,1)}, bf16[16,8,128]{2,1,0:T(8,128)(2,1)S(1)}, u32[]{:S(2)}) copy-start(bf16[16,8,128]{2,1,0:T(8,128)(2,1)S(1)} %scatter.21) | copy-start | bytes 98308
  16.5 100.0 %copy-start.17 = (f32[16,256]{1,0:T(8,128)}, f32[16,256]{1,0:T(8,128)S(1)}, u32[]{:S(2)}) copy-start(f32[16,256]{1,0:T(8,128)S(1)} %copy_bitcast_fusion.2) | copy-start | bytes 49156
  16.7 35.1 %copy-start.25 = (f32[16]{0:T(128)}, f32[16]{0:T(128)S(1)}, u32[]{:S(2)}) copy-start(f32[16]{0:T(128)S(1)} %slice_reduce_fusion.4) | copy-start | bytes 196
  17.5 37.2 %copy-start.14 = (f32[256,16]{0,1:T(8,128)}, f32[256,16]{0,1:T(8,128)S(1)}, u32[]{:S(2)}) copy-start(f32[256,16]{0,1:T(8,128)S(1)} %get-tuple-element.170) | copy-start | bytes 49156
  17.5 99.1 %copy-start.12 = (f32[256,16]{0,1:T(8,128)}, f32[256,16]{0,1:T(8,128)S(1)}, u32[]{:S(2)}) copy-start(f32[256,16]{0,1:T(8,128)S(1)} %get-tuple-element.169) | copy-start | bytes 49156
  18.8 49.0 %copy-start.6 = (bf16[256,128]{1,0:T(8,128)(2,1)S(1)}, bf16[256,128]{1,0:T(8,128)(2,1)}, u32[]{:S(2)}) copy-start(bf16[256,128]{1,0:T(8,128)(2,1)} %param.26) | copy-start | bytes 196612
  18.8 49.0 %copy-start.7 = (bf16[256,128]{1,0:T(8,128)(2,1)S(1)}, bf16[256,128]{1,0:T(8,128)(2,1)}, u32[]{:S(2)}) copy-start(bf16[256,128]{1,0:T(8,128)(2,1)} %param.27) | copy-start | bytes 196612
  18.8 24.7 %collective-permute-start = (bf16[16,72,128]{2,1,0:T(8,128)(2,1)}, bf16[16,72,128]{2,1,0:T(8,128)(2,1)}, u32[]{:S(2)}, u32[]{:S(2)}) collective-permute-start(bf16[16,72,128]{2,1,0:T(8,128)(2,1)} %pad_maximum_fusion.1), channel_id=1, source_target_pairs={{0,8},{8,16},{16,24},{24,32},{32,40},{40,48},{48,56},{56,64},{64,7... | collective-permute-start | bytes 884744 | tf_op jit(solution)/shard_map/ppermute | solution.py:16
  21.0 23.6 %collective-permute-start.1 = (bf16[16,72,128]{2,1,0:T(8,128)(2,1)}, bf16[16,72,128]{2,1,0:T(8,128)(2,1)}, u32[]{:S(2)}, u32[]{:S(2)}) collective-permute-start(bf16[16,72,128]{2,1,0:T(8,128)(2,1)} %pad_maximum_fusion.1), channel_id=1, source_target_pairs={{0,16},{8,24},{16,32},{24,40},{32,48},{40,56},{48,64},{56,72},{64,... | collective-permute-start | bytes 884744 | tf_op jit(solution)/shard_map/ppermute | solution.py:16
  25.1 20.5 %collective-permute-start.3 = (bf16[16,72,128]{2,1,0:T(8,128)(2,1)}, bf16[16,72,128]{2,1,0:T(8,128)(2,1)}, u32[]{:S(2)}, u32[]{:S(2)}) collective-permute-start(bf16[16,72,128]{2,1,0:T(8,128)(2,1)} %pad_maximum_fusion.1), channel_id=1, source_target_pairs={{0,32},{8,40},{16,48},{24,56},{32,64},{40,72},{48,80},{56,88},{64,... | collective-permute-start | bytes 884744 | tf_op jit(solution)/shard_map/ppermute | solution.py:16
  29.8 22.0 %collective-permute-start.2 = (bf16[16,72,128]{2,1,0:T(8,128)(2,1)}, bf16[16,72,128]{2,1,0:T(8,128)(2,1)}, u32[]{:S(2)}, u32[]{:S(2)}) collective-permute-start(bf16[16,72,128]{2,1,0:T(8,128)(2,1)} %pad_maximum_fusion.1), channel_id=1, source_target_pairs={{0,24},{8,32},{16,40},{24,48},{32,56},{40,64},{48,72},{56,80},{64,... | collective-permute-start | bytes 884744 | tf_op jit(solution)/shard_map/ppermute | solution.py:16
  38.1 83.5 %all-to-all-start.1 = ((bf16[256,8,512]{2,0,1:T(8,128)(2,1)}), bf16[256,8,512]{2,0,1:T(8,128)(2,1)S(1)}, u32[]{:S(2)}, u32[]{:S(2)}) async-start(bf16[256,8,512]{2,0,1:T(8,128)(2,1)} %broadcast_in_dim.22), calls=%async_computation.1 | async-start | bytes 4194304 | tf_op jit(solution)/shard_map/all_to_all | solution.py:61
  54.7 59.3 %collective-permute-start.5 = (bf16[16,72,128]{2,1,0:T(8,128)(2,1)S(1)}, bf16[16,72,128]{2,1,0:T(8,128)(2,1)S(1)}, u32[]{:S(2)}, u32[]{:S(2)}) collective-permute-start(bf16[16,72,128]{2,1,0:T(8,128)(2,1)S(1)} %pad_maximum_fusion.2), channel_id=1, source_target_pairs={{0,64},{8,72},{16,80},{24,88},{32,96},{40,104},{48,112},{56,120},{... | collective-permute-start | bytes 884744 | tf_op jit(solution)/shard_map/ppermute | solution.py:16
  64.8 49.2 %collective-permute-start.4 = (bf16[16,72,128]{2,1,0:T(8,128)(2,1)S(1)}, bf16[16,72,128]{2,1,0:T(8,128)(2,1)S(1)}, u32[]{:S(2)}, u32[]{:S(2)}) collective-permute-start(bf16[16,72,128]{2,1,0:T(8,128)(2,1)S(1)} %pad_maximum_fusion.2), channel_id=1, source_target_pairs={{0,32},{8,40},{16,48},{24,56},{32,64},{40,72},{48,80},{56,88},{64,... | collective-permute-start | bytes 884744 | tf_op jit(solution)/shard_map/ppermute | solution.py:16
  68.0 52.0 %copy-start.10 = (f32[256,256]{1,0:T(8,128)}, f32[256,256]{1,0:T(8,128)S(1)}, u32[]{:S(2)}) copy-start(f32[256,256]{1,0:T(8,128)S(1)} %fusion.107) | copy-start | bytes 786436
  68.0 46.2 %collective-permute-start.6 = (bf16[16,72,128]{2,1,0:T(8,128)(2,1)S(1)}, bf16[16,72,128]{2,1,0:T(8,128)(2,1)S(1)}, u32[]{:S(2)}, u32[]{:S(2)}) collective-permute-start(bf16[16,72,128]{2,1,0:T(8,128)(2,1)S(1)} %pad_maximum_fusion.2), channel_id=1, source_target_pairs={{0,96},{8,104},{16,112},{24,120},{1,97},{9,105},{17,113},{25,121},... | collective-permute-start | bytes 884744 | tf_op jit(solution)/shard_map/ppermute | solution.py:16
  69.5 50.5 %copy-start.16 = (pred[256,256]{1,0:T(8,128)(4,1)}, pred[256,256]{1,0:T(8,128)(4,1)S(1)}, u32[]{:S(2)}) copy-start(pred[256,256]{1,0:T(8,128)(4,1)S(1)} %fusion.61) | copy-start | bytes 196612
  136.4 32.6 %all-to-all-start = ((bf16[256,8,512]{2,0,1:T(8,128)(2,1)}), bf16[256,8,512]{2,0,1:T(8,128)(2,1)S(1)}, u32[]{:S(2)}, u32[]{:S(2)}) async-start(bf16[256,8,512]{2,0,1:T(8,128)(2,1)} %bitcast.128), calls=%async_computation | async-start | bytes 4194304 | tf_op jit(solution)/shard_map/all_to_all | solution.py:69
  169.0 186.2 %all-to-all-start.2 = ((bf16[16,256,1024]{1,2,0:T(8,128)(2,1)}), bf16[16,256,1024]{1,2,0:T(8,128)(2,1)}, u32[]{:S(2)}, u32[]{:S(2)}) async-start(bf16[16,256,1024]{1,2,0:T(8,128)(2,1)} %bitcast.122), calls=%async_computation.2 | async-start | bytes 16777216 | tf_op jit(solution)/shard_map/all_to_all | solution.py:183
  182.9 15.5 %collective-permute-start.7 = (bf16[16,72,128]{2,1,0:T(8,128)(2,1)}, bf16[16,72,128]{2,1,0:T(8,128)(2,1)}, u32[]{:S(2)}, u32[]{:S(2)}) collective-permute-start(bf16[16,72,128]{2,1,0:T(8,128)(2,1)} %pad_maximum_fusion), channel_id=1, source_target_pairs={{8,0},{16,8},{24,16},{32,24},{40,32},{48,40},{56,48},{64,56},{72,6... | collective-permute-start | bytes 884744 | tf_op jit(solution)/shard_map/ppermute | solution.py:16
  192.0 91.6 %collective-permute-start.10 = (bf16[16,72,128]{2,1,0:T(8,128)(2,1)}, bf16[16,72,128]{2,1,0:T(8,128)(2,1)}, u32[]{:S(2)}, u32[]{:S(2)}) collective-permute-start(bf16[16,72,128]{2,1,0:T(8,128)(2,1)} %pad_maximum_fusion), channel_id=1, source_target_pairs={{32,0},{40,8},{48,16},{56,24},{64,32},{72,40},{80,48},{88,56},{96,... | collective-permute-start | bytes 884744 | tf_op jit(solution)/shard_map/ppermute | solution.py:16
  193.3 90.3 %collective-permute-start.9 = (bf16[16,72,128]{2,1,0:T(8,128)(2,1)}, bf16[16,72,128]{2,1,0:T(8,128)(2,1)}, u32[]{:S(2)}, u32[]{:S(2)}) collective-permute-start(bf16[16,72,128]{2,1,0:T(8,128)(2,1)} %pad_maximum_fusion), channel_id=1, source_target_pairs={{24,0},{32,8},{40,16},{48,24},{56,32},{64,40},{72,48},{80,56},{88,... | collective-permute-start | bytes 884744 | tf_op jit(solution)/shard_map/ppermute | solution.py:16
  194.6 87.9 %collective-permute-start.8 = (bf16[16,72,128]{2,1,0:T(8,128)(2,1)}, bf16[16,72,128]{2,1,0:T(8,128)(2,1)}, u32[]{:S(2)}, u32[]{:S(2)}) collective-permute-start(bf16[16,72,128]{2,1,0:T(8,128)(2,1)} %pad_maximum_fusion), channel_id=1, source_target_pairs={{16,0},{24,8},{32,16},{40,24},{48,32},{56,40},{64,48},{72,56},{80,... | collective-permute-start | bytes 884744 | tf_op jit(solution)/shard_map/ppermute | solution.py:16
  284.9 53.4 %copy-start.15 = (f32[256,16]{0,1:T(8,128)S(1)}, f32[256,16]{0,1:T(8,128)}, u32[]{:S(2)}) copy-start(f32[256,16]{0,1:T(8,128)} %copy-done.14) | copy-start | bytes 49156
  284.9 53.4 %copy-start.18 = (f32[16,256]{1,0:T(8,128)S(1)}, f32[16,256]{1,0:T(8,128)}, u32[]{:S(2)}) copy-start(f32[16,256]{1,0:T(8,128)} %copy-done.17) | copy-start | bytes 49156
  287.9 22.6 %collective-permute-start.12 = (bf16[16,72,128]{2,1,0:T(8,128)(2,1)}, bf16[16,72,128]{2,1,0:T(8,128)(2,1)}, u32[]{:S(2)}, u32[]{:S(2)}) collective-permute-start(bf16[16,72,128]{2,1,0:T(8,128)(2,1)} %pad_maximum_fusion.3), channel_id=1, source_target_pairs={{64,0},{72,8},{80,16},{88,24},{96,32},{104,40},{112,48},{120,56},{... | collective-permute-start | bytes 884744 | tf_op jit(solution)/shard_map/ppermute | solution.py:16
  289.2 36.5 %collective-permute-start.11 = (bf16[16,72,128]{2,1,0:T(8,128)(2,1)}, bf16[16,72,128]{2,1,0:T(8,128)(2,1)}, u32[]{:S(2)}, u32[]{:S(2)}) collective-permute-start(bf16[16,72,128]{2,1,0:T(8,128)(2,1)} %pad_maximum_fusion.3), channel_id=1, source_target_pairs={{32,0},{40,8},{48,16},{56,24},{64,32},{72,40},{80,48},{88,56},{96,... | collective-permute-start | bytes 884744 | tf_op jit(solution)/shard_map/ppermute | solution.py:16
  290.7 46.4 %copy-start.1 = (bf16[256,1024]{0,1:T(8,128)(2,1)S(1)}, bf16[256,1024]{0,1:T(8,128)(2,1)}, u32[]{:S(2)}) copy-start(bf16[256,1024]{0,1:T(8,128)(2,1)} %copy-done) | copy-start | bytes 1572868
  290.7 47.6 %copy-start.11 = (f32[256,256]{1,0:T(8,128)S(1)}, f32[256,256]{1,0:T(8,128)}, u32[]{:S(2)}) copy-start(f32[256,256]{1,0:T(8,128)} %copy-done.10) | copy-start | bytes 786436
  290.7 44.1 %collective-permute-start.13 = (bf16[16,72,128]{2,1,0:T(8,128)(2,1)}, bf16[16,72,128]{2,1,0:T(8,128)(2,1)S(1)}, u32[]{:S(2)}, u32[]{:S(2)}) collective-permute-start(bf16[16,72,128]{2,1,0:T(8,128)(2,1)} %pad_maximum_fusion.3), channel_id=1, source_target_pairs={{96,0},{104,8},{112,16},{120,24},{97,1},{105,9},{113,17},{121,25},... | collective-permute-start | bytes 884744 | tf_op jit(solution)/shard_map/ppermute | solution.py:16
  (19 other events, 199.6 us)
Sparse Core Ops, SparseCore 0:
  10.4 97.4 all-gather.1

commit v3 on v1

--- a/solution.py
+++ b/solution.py
@@ -142,7 +142,6 @@
     b_float = inputs_b.astype(jnp.float32)
     c_float = inputs_c.astype(jnp.float32)
     z_float = gate_z.astype(jnp.float32)
-    heads_here = log_decay.shape[0]
 
     assert inputs_x.shape[0] == SPAN
 
@@ -175,15 +174,14 @@
     )
     layer_out = head_sum_scatter(partial_value.astype(jnp.bfloat16)).astype(jnp.bfloat16)
     grad_full = head_gather(out_grad)
-    grad_y = jnp.dot(grad_full, full_weight, preferred_element_type=jnp.float32)
+    weight_term = lax.dot_general(
+        grad_full, normed_bf, (((0,), (0,)), ((), ())), preferred_element_type=jnp.float32
+    ).astype(jnp.bfloat16)
     grad_weight = lax.psum_scatter(
-        lax.dot_general(
-            grad_full, normed_bf, (((0,), (0,)), ((), ())), preferred_element_type=jnp.float32
-        ).astype(jnp.bfloat16),
-        "seq",
-        scatter_dimension=0,
-        tiled=True,
+        weight_term, "seq", scatter_dimension=0, tiled=True
     ).astype(jnp.float32)
+    after_term = grad_full + weight_term[0, 0] * jnp.zeros((), jnp.bfloat16)
+    grad_y = jnp.dot(after_term, full_weight, preferred_element_type=jnp.float32)
     d_zero, d_c_two, d_decay_two, grad_z, adjoint_in = pull_finish(grad_y)
 
     adjoint_out = prefix_combine(g_local, adjoint_in, -1)

time: 272 us -> 384 us (1.41)
  waiting for transfers between devices: 104 us -> 221 us
    reduce_scatter x1, waiting for transfers between devices: 6.1 us -> 100 us  [per_device(): lax.psum_scatter(weight_term, 'seq', scatter_dimension=0, tiled=True)]
    all_gather x1, waiting for transfers between devices: 0.01 us -> 71.8 us  [per_device(): full_weight = lax.all_gather(out_weight, 'seq', axis=0, tiled=True)]
    ppermute x14, waiting for transfers between devices: 96.8 us -> 47.8 us  [from_behind(): lax.ppermute(value, axis, [(source, source + steps) for source in range(l...]
  transfers between devices with their start and end apart: 18 -> 18, of which waited for: 7 -> 8; matrix products, arithmetic and copies ran while one was open for 31% -> 15% of each run, Pallas kernels for 0% -> 0%
where the time goes in v3:
time: 384 us; the launch traced here: 382 us
  waiting for transfers between devices  221 us (58%)
  starting transfers between devices  48.2 us (13%)
  matrix products  41.7 us (11%)
  other arithmetic  33.6 us (9%)
  local copies, waits for them, and re-layouts  21.8 us (6%)
  between operations  16.1 us (4%)
    reduce_scatter x1, waiting for transfers between devices, per_device(): lax.psum_scatter(weight_term, 'seq', scatter_dimension=0, tiled=True)  100 us
    all_gather x1, waiting for transfers between devices, per_device(): full_weight = lax.all_gather(out_weight, 'seq', axis=0, tiled=True)  71.8 us
    ppermute x14, waiting for transfers between devices, from_behind(): lax.ppermute(value, axis, [(source, source + steps) for source in range(l...  47.8 us
    ppermute x14, starting transfers between devices, from_behind(): lax.ppermute(value, axis, [(source, source + steps) for source in range(l...  37.9 us
    dot_general x3, matrix products, block_outputs(): jnp.einsum('hts,shp->thp', scores, x_heads, precision=lax.Precision.HIGH)  13.1 us
    another operation x11, other arithmetic  9.32 us
  transfers between devices with their start and end apart: 18, of which 8 were waited for; matrix products, arithmetic and copies ran while one was open for 15% of the time, Pallas kernels for 0%

profile of v3, /device:TPU:0, one launch (start us, length us, event | category | flops | bytes accessed | tf_op | source)
XLA Modules:
  0.0 382.0 jit_solution(7875643703704706678)
XLA Ops:
  19.0 4.1 %collective-permute-start.1 = (bf16[16,72,128]{2,1,0:T(8,128)(2,1)S(1)}, bf16[16,72,128]{2,1,0:T(8,128)(2,1)S(1)}, u32[]{:S(2)}, u32[]{:S(2)}) collective-permute-start(bf16[16,72,128]{2,1,0:T(8,128)(2,1)S(1)} %pad_maximum_fusion.1), channel_id=1, source_target_pairs={{0,16},{8,24},{16,32},{24,40},{32,48},{40,56},{48,64},{56,72},{64,... | collective-permute-start | bytes 884744 | tf_op jit(solution)/shard_map/ppermute | solution.py:16
  23.1 4.0 %collective-permute-start.2 = (bf16[16,72,128]{2,1,0:T(8,128)(2,1)S(1)}, bf16[16,72,128]{2,1,0:T(8,128)(2,1)S(1)}, u32[]{:S(2)}, u32[]{:S(2)}) collective-permute-start(bf16[16,72,128]{2,1,0:T(8,128)(2,1)S(1)} %pad_maximum_fusion.1), channel_id=1, source_target_pairs={{0,24},{8,32},{16,40},{24,48},{32,56},{40,64},{48,72},{56,80},{64,... | collective-permute-start | bytes 884744 | tf_op jit(solution)/shard_map/ppermute | solution.py:16
  27.1 6.5 %collective-permute-start.3 = (bf16[16,72,128]{2,1,0:T(8,128)(2,1)S(1)}, bf16[16,72,128]{2,1,0:T(8,128)(2,1)S(1)}, u32[]{:S(2)}, u32[]{:S(2)}) collective-permute-start(bf16[16,72,128]{2,1,0:T(8,128)(2,1)S(1)} %pad_maximum_fusion.1), channel_id=1, source_target_pairs={{0,32},{8,40},{16,48},{24,56},{32,64},{40,72},{48,80},{56,88},{64,... | collective-permute-start | bytes 884744 | tf_op jit(solution)/shard_map/ppermute | solution.py:16
  33.7 2.4 broadcast_in_dim.22
  36.1 5.4 %all-to-all-start.1 = ((bf16[256,8,512]{2,0,1:T(8,128)(2,1)}), bf16[256,8,512]{2,0,1:T(8,128)(2,1)}, u32[]{:S(2)}, u32[]{:S(2)}) async-start(bf16[256,8,512]{2,0,1:T(8,128)(2,1)} %broadcast_in_dim.22), calls=%async_computation.1 | async-start | bytes 4194304 | tf_op jit(solution)/shard_map/all_to_all | solution.py:61
  44.0 5.9 %collective-permute-start.4 = (bf16[16,72,128]{2,1,0:T(8,128)(2,1)S(1)}, bf16[16,72,128]{2,1,0:T(8,128)(2,1)S(1)}, u32[]{:S(2)}, u32[]{:S(2)}) collective-permute-start(bf16[16,72,128]{2,1,0:T(8,128)(2,1)S(1)} %pad_maximum_fusion.2), channel_id=1, source_target_pairs={{0,32},{8,40},{16,48},{24,56},{32,64},{40,72},{48,80},{56,88},{64,... | collective-permute-start | bytes 884744 | tf_op jit(solution)/shard_map/ppermute | solution.py:16
  49.9 5.1 %collective-permute-start.5 = (bf16[16,72,128]{2,1,0:T(8,128)(2,1)S(1)}, bf16[16,72,128]{2,1,0:T(8,128)(2,1)S(1)}, u32[]{:S(2)}, u32[]{:S(2)}) collective-permute-start(bf16[16,72,128]{2,1,0:T(8,128)(2,1)S(1)} %pad_maximum_fusion.2), channel_id=1, source_target_pairs={{0,64},{8,72},{16,80},{24,88},{32,96},{40,104},{48,112},{56,120},{... | collective-permute-start | bytes 884744 | tf_op jit(solution)/shard_map/ppermute | solution.py:16
  56.8 26.7 %collective-permute-done.5 = bf16[16,72,128]{2,1,0:T(8,128)(2,1)S(1)} collective-permute-done((bf16[16,72,128]{2,1,0:T(8,128)(2,1)S(1)}, bf16[16,72,128]{2,1,0:T(8,128)(2,1)S(1)}, u32[]{:S(2)}, u32[]{:S(2)}) %collective-permute-start.5) | collective-permute-done | bytes 294944 | tf_op jit(solution)/shard_map/ppermute | solution.py:16
  85.2 3.4 fusion.32
  90.6 3.9 %copy.74 = bf16[256,8,512]{0,2,1:T(8,128)(2,1)} copy(bf16[256,8,512]{2,0,1:T(8,128)(2,1)} %all-to-all-done.1) | data formatting | bytes 4194304 | tf_op jit(solution)/shard_map/all_to_all | solution.py:61
  94.6 7.5 %convert_bitcast_fusion = bf16[4096,1024]{0,1:T(8,128)(2,1)} fusion(bf16[256,4096]{0,1:T(8,128)(2,1)} %bitcast.129, f32[1024]{0:T(1024)S(1)} %copy-done.34, f32[256]{0:T(256)S(1)} %fusion.91, f32[256,1024]{1,0:T(8,128)S(1)} %copy.72, bf16[256,1024]{1,0:T(8,128)(2,1)S(1)} %copy-done.6), kind=kOutput, calls=%fused_computation | convolution fusion | flops 2154037248 | bytes 12063744 | tf_op jit(solution)/shard_map/dot_general | solution.py:177
  104.7 100.4 %reduce-scatter.2.cloned.1.call-done = bf16[256,1024]{0,1:T(8,128)(2,1)} async-done(((bf16[4096,1024]{0,1:T(8,128)(2,1)}), bf16[256,1024]{0,1:T(8,128)(2,1)}) %reduce-scatter.2.cloned.1.call-update) | async-done | bytes 524304 | tf_op jit(solution)/shard_map/reduce_scatter | solution.py:180
  205.1 2.2 copy.83
  207.3 71.8 %all-gather.2.cloned.1.call-done = bf16[4096,1024]{1,0:T(8,128)(2,1)} async-done(((bf16[256,1024]{1,0:T(8,128)(2,1)}), bf16[4096,1024]{1,0:T(8,128)(2,1)}) %all-gather.2.cloned.1.call-update) | async-done | bytes 8388624 | tf_op jit(solution)/shard_map/all_gather | solution.py:171
  279.2 6.6 %multiply_reduce_fusion.1 = (f32[256]{0:T(256)S(1)}, f32[256,1024]{1,0:T(8,128)S(1)}) fusion(f32[256,1024]{1,0:T(8,128)S(1)} %copy.72, bf16[256,1024]{1,0:T(8,128)(2,1)S(1)} %copy-done.6, f32[1024]{0:T(1024)S(1)} %copy-done.34, bf16[4096,1024]{1,0:T(8,128)(2,1)} %all-gather.2.cloned.1.call-done, bf16[256,4096]{0,1:T(8,128)(2,1)} %bitcast.130, bf16[]{:T(256)} %bitcast.11), kind=kOutput, calls=%fused_computation.58 | convolution fusion | flops 2150891264 | bytes 13112322 | tf_op jit(solution)/shard_map/dot_general | solution.py:184
  285.8 2.1 fusion.49
  297.6 5.3 %fusion.60 = (f32[16,256]{1,0:T(8,128)S(1)}, f32[16,256]{1,0:T(8,128)S(1)}, f32[256,256]{1,0:T(8,128)S(1)}) fusion(f32[16,256]{1,0:T(8,128)} %copy-done.18, f32[256,256]{1,0:T(8,128)} %copy-done.11, pred[256,256]{1,0:T(8,128)(4,1)} %copy-done.16, f32[16,64,256]{2,1,0:T(8,128)S(1)} %bitcast.120, bf16[256,16,64]{0,2,1:T(8,128)(2,1)S(1)} %bitcast.126), kind=kOutput, calls=%fused_computation.69 | convolution fusion | flops 418308096 | bytes 2211840 | tf_op jit(solution)/shard_map/transpose(jvp(hts,shp->thp))/dot_general | solution.py:95
  304.9 3.9 %convolution_convert_fusion = bf16[256,4096]{1,0:T(8,128)(2,1)} fusion(bf16[4096,1024]{1,0:T(8,128)(2,1)S(1)} %bitcast.136, f32[1024]{0:T(1024)S(1)} %copy-done.35, f32[256]{0:T(256)S(1)} %copy-done.32, f32[256,1024]{1,0:T(8,128)S(1)} %copy.72, bf16[256,1024]{1,0:T(8,128)(2,1)S(1)} %copy-done.7), kind=kOutput, calls=%fused_computation.4 | convolution fusion | flops 2150891520 | bytes 12063744 | tf_op jit(solution)/shard_map/dot_general | solution.py:172
  309.2 2.5 reduce-window.41
  313.8 2.1 multiply_reduce_fusion.4
  316.2 2.3 fusion.99
  324.1 4.6 %all-to-all-start = ((bf16[256,8,512]{2,0,1:T(8,128)(2,1)}), bf16[256,8,512]{2,0,1:T(8,128)(2,1)S(1)}, u32[]{:S(2)}, u32[]{:S(2)}) async-start(bf16[256,8,512]{2,0,1:T(8,128)(2,1)} %bitcast.123), calls=%async_computation | async-start | bytes 4194304 | tf_op jit(solution)/shard_map/all_to_all | solution.py:69
  331.7 2.8 collective-permute-done.11
  334.5 5.4 %collective-permute-done.12 = bf16[16,72,128]{2,1,0:T(8,128)(2,1)} collective-permute-done((bf16[16,72,128]{2,1,0:T(8,128)(2,1)}, bf16[16,72,128]{2,1,0:T(8,128)(2,1)}, u32[]{:S(2)}, u32[]{:S(2)}) %collective-permute-start.12) | collective-permute-done | bytes 294944 | tf_op jit(solution)/shard_map/ppermute | solution.py:16
  341.1 11.7 %collective-permute-done.13 = bf16[16,72,128]{2,1,0:T(8,128)(2,1)S(1)} collective-permute-done((bf16[16,72,128]{2,1,0:T(8,128)(2,1)}, bf16[16,72,128]{2,1,0:T(8,128)(2,1)S(1)}, u32[]{:S(2)}, u32[]{:S(2)}) %collective-permute-start.13) | collective-permute-done | bytes 294944 | tf_op jit(solution)/shard_map/ppermute | solution.py:16
  352.8 2.3 multiply_reduce_fusion.3
  355.0 2.2 fusion.44
  358.3 2.5 reduce-window.45
  360.9 2.5 reduce-window.49
  363.6 4.4 %fusion.35 = f32[256,16,64]{0,2,1:T(8,128)} fusion(f32[16,64,256]{2,1,0:T(8,128)S(1)} %bitcast.122, f32[16,256]{1,0:T(8,128)} %copy-done.18, f32[256,256]{1,0:T(8,128)} %copy-done.11, pred[256,256]{1,0:T(8,128)(4,1)S(1)} %copy-done.17, f32[256,16,64]{0,2,1:T(8,128)} %get-tuple-element.178, f32[256,16]{0,1:T(8,128)S(1)} %copy-done.15), kind=kOutput, calls=%fused_computation.38 | convolution fusion | flops 407371776 | bytes 3506176 | tf_op jit(solution)/shard_map/transpose(jvp(hts,shp->thp))/dot_general | solution.py:95
  368.0 2.5 copy.82
  371.2 2.9 fusion.43
  (183 shorter events, 47.7 us)
Async XLA Ops:
  9.6 75.6 %copy-start.18 = (f32[16,256]{1,0:T(8,128)}, f32[16,256]{1,0:T(8,128)S(1)}, u32[]{:S(2)}) copy-start(f32[16,256]{1,0:T(8,128)S(1)} %copy_bitcast_fusion.1) | copy-start | bytes 49156
  14.9 282.7 %copy-start = (bf16[256,1024]{0,1:T(8,128)(2,1)}, bf16[256,1024]{0,1:T(8,128)(2,1)S(1)}, u32[]{:S(2)}) copy-start(bf16[256,1024]{0,1:T(8,128)(2,1)S(1)} %copy.71) | copy-start | bytes 1572868
  16.7 68.5 %copy-start.12 = (f32[256,16]{0,1:T(8,128)}, f32[256,16]{0,1:T(8,128)S(1)}, u32[]{:S(2)}) copy-start(f32[256,16]{0,1:T(8,128)S(1)} %get-tuple-element.167) | copy-start | bytes 49156
  17.5 37.5 %copy-start.8 = (bf16[256,128]{1,0:T(8,128)(2,1)S(1)}, bf16[256,128]{1,0:T(8,128)(2,1)}, u32[]{:S(2)}) copy-start(bf16[256,128]{1,0:T(8,128)(2,1)} %param.26) | copy-start | bytes 196612
  17.5 37.5 %copy-start.9 = (bf16[256,128]{1,0:T(8,128)(2,1)S(1)}, bf16[256,128]{1,0:T(8,128)(2,1)}, u32[]{:S(2)}) copy-start(bf16[256,128]{1,0:T(8,128)(2,1)} %param.27) | copy-start | bytes 196612
  17.5 24.1 %collective-permute-start = (bf16[16,72,128]{2,1,0:T(8,128)(2,1)S(1)}, bf16[16,72,128]{2,1,0:T(8,128)(2,1)S(1)}, u32[]{:S(2)}, u32[]{:S(2)}) collective-permute-start(bf16[16,72,128]{2,1,0:T(8,128)(2,1)S(1)} %pad_maximum_fusion.1), channel_id=1, source_target_pairs={{0,8},{8,16},{16,24},{24,32},{32,40},{40,48},{48,56},{56,64},{64,7... | collective-permute-start | bytes 884744 | tf_op jit(solution)/shard_map/ppermute | solution.py:16
  19.0 22.9 %collective-permute-start.1 = (bf16[16,72,128]{2,1,0:T(8,128)(2,1)S(1)}, bf16[16,72,128]{2,1,0:T(8,128)(2,1)S(1)}, u32[]{:S(2)}, u32[]{:S(2)}) collective-permute-start(bf16[16,72,128]{2,1,0:T(8,128)(2,1)S(1)} %pad_maximum_fusion.1), channel_id=1, source_target_pairs={{0,16},{8,24},{16,32},{24,40},{32,48},{40,56},{48,64},{56,72},{64,... | collective-permute-start | bytes 884744 | tf_op jit(solution)/shard_map/ppermute | solution.py:16
  23.1 18.9 %collective-permute-start.2 = (bf16[16,72,128]{2,1,0:T(8,128)(2,1)S(1)}, bf16[16,72,128]{2,1,0:T(8,128)(2,1)S(1)}, u32[]{:S(2)}, u32[]{:S(2)}) collective-permute-start(bf16[16,72,128]{2,1,0:T(8,128)(2,1)S(1)} %pad_maximum_fusion.1), channel_id=1, source_target_pairs={{0,24},{8,32},{16,40},{24,48},{32,56},{40,64},{48,72},{56,80},{64,... | collective-permute-start | bytes 884744 | tf_op jit(solution)/shard_map/ppermute | solution.py:16
  27.1 16.0 %collective-permute-start.3 = (bf16[16,72,128]{2,1,0:T(8,128)(2,1)S(1)}, bf16[16,72,128]{2,1,0:T(8,128)(2,1)S(1)}, u32[]{:S(2)}, u32[]{:S(2)}) collective-permute-start(bf16[16,72,128]{2,1,0:T(8,128)(2,1)S(1)} %pad_maximum_fusion.1), channel_id=1, source_target_pairs={{0,32},{8,40},{16,48},{24,56},{32,64},{40,72},{48,80},{56,88},{64,... | collective-permute-start | bytes 884744 | tf_op jit(solution)/shard_map/ppermute | solution.py:16
  36.1 54.5 %all-to-all-start.1 = ((bf16[256,8,512]{2,0,1:T(8,128)(2,1)}), bf16[256,8,512]{2,0,1:T(8,128)(2,1)}, u32[]{:S(2)}, u32[]{:S(2)}) async-start(bf16[256,8,512]{2,0,1:T(8,128)(2,1)} %broadcast_in_dim.22), calls=%async_computation.1 | async-start | bytes 4194304 | tf_op jit(solution)/shard_map/all_to_all | solution.py:61
  41.6 163.5 %reduce-scatter.2.cloned.1.call-start = ((), (), s32[]{:S(2)}) async-start(), calls=%async_computation.4 | async-start | bytes 8912896 | tf_op jit(solution)/shard_map/reduce_scatter | solution.py:180
  44.0 12.8 %collective-permute-start.4 = (bf16[16,72,128]{2,1,0:T(8,128)(2,1)S(1)}, bf16[16,72,128]{2,1,0:T(8,128)(2,1)S(1)}, u32[]{:S(2)}, u32[]{:S(2)}) collective-permute-start(bf16[16,72,128]{2,1,0:T(8,128)(2,1)S(1)} %pad_maximum_fusion.2), channel_id=1, source_target_pairs={{0,32},{8,40},{16,48},{24,56},{32,64},{40,72},{48,80},{56,88},{64,... | collective-permute-start | bytes 884744 | tf_op jit(solution)/shard_map/ppermute | solution.py:16
  49.9 33.6 %collective-permute-start.5 = (bf16[16,72,128]{2,1,0:T(8,128)(2,1)S(1)}, bf16[16,72,128]{2,1,0:T(8,128)(2,1)S(1)}, u32[]{:S(2)}, u32[]{:S(2)}) collective-permute-start(bf16[16,72,128]{2,1,0:T(8,128)(2,1)S(1)} %pad_maximum_fusion.2), channel_id=1, source_target_pairs={{0,64},{8,72},{16,80},{24,88},{32,96},{40,104},{48,112},{56,120},{... | collective-permute-start | bytes 884744 | tf_op jit(solution)/shard_map/ppermute | solution.py:16
  55.2 33.3 %copy-start.11 = (f32[256,256]{1,0:T(8,128)}, f32[256,256]{1,0:T(8,128)S(1)}, u32[]{:S(2)}) copy-start(f32[256,256]{1,0:T(8,128)S(1)} %fusion.113) | copy-start | bytes 786436
  55.3 28.4 %collective-permute-start.6 = (bf16[16,72,128]{2,1,0:T(8,128)(2,1)S(1)}, bf16[16,72,128]{2,1,0:T(8,128)(2,1)S(1)}, u32[]{:S(2)}, u32[]{:S(2)}) collective-permute-start(bf16[16,72,128]{2,1,0:T(8,128)(2,1)S(1)} %pad_maximum_fusion.2), channel_id=1, source_target_pairs={{0,96},{8,104},{16,112},{24,120},{1,97},{9,105},{17,113},{25,121},... | collective-permute-start | bytes 884744 | tf_op jit(solution)/shard_map/ppermute | solution.py:16
  56.7 31.9 %copy-start.16 = (pred[256,256]{1,0:T(8,128)(4,1)}, pred[256,256]{1,0:T(8,128)(4,1)S(1)}, u32[]{:S(2)}) copy-start(pred[256,256]{1,0:T(8,128)(4,1)S(1)} %fusion.67) | copy-start | bytes 196612
  83.9 219.2 %copy-start.2 = (f32[16,64,128]{2,1,0:T(8,128)}, f32[16,64,128]{2,1,0:T(8,128)S(1)}, u32[]{:S(2)}) copy-start(f32[16,64,128]{2,1,0:T(8,128)S(1)} %multiply_add_fusion.2) | copy-start | bytes 1572868
  90.6 195.2 %copy-start.31 = (f32[256]{0:T(256)}, f32[256]{0:T(256)S(1)}, u32[]{:S(2)}) copy-start(f32[256]{0:T(256)S(1)} %fusion.91) | copy-start | bytes 3076
  102.1 177.0 %all-gather.2.cloned.1.call-start = ((), (), s32[]{:S(2)}) async-start(), calls=%async_computation.3 | async-start | bytes 8912896 | tf_op jit(solution)/shard_map/all_gather | solution.py:171
  292.4 19.3 %collective-permute-start.7 = (bf16[16,72,128]{2,1,0:T(8,128)(2,1)}, bf16[16,72,128]{2,1,0:T(8,128)(2,1)}, u32[]{:S(2)}, u32[]{:S(2)}) collective-permute-start(bf16[16,72,128]{2,1,0:T(8,128)(2,1)} %pad_maximum_fusion), channel_id=1, source_target_pairs={{8,0},{16,8},{24,16},{32,24},{40,32},{48,40},{56,48},{64,56},{72,6... | collective-permute-start | bytes 884744 | tf_op jit(solution)/shard_map/ppermute | solution.py:16
  293.7 19.1 %collective-permute-start.8 = (bf16[16,72,128]{2,1,0:T(8,128)(2,1)}, bf16[16,72,128]{2,1,0:T(8,128)(2,1)}, u32[]{:S(2)}, u32[]{:S(2)}) collective-permute-start(bf16[16,72,128]{2,1,0:T(8,128)(2,1)} %pad_maximum_fusion), channel_id=1, source_target_pairs={{16,0},{24,8},{32,16},{40,24},{48,32},{56,40},{64,48},{72,56},{80,... | collective-permute-start | bytes 884744 | tf_op jit(solution)/shard_map/ppermute | solution.py:16
  295.0 18.9 %collective-permute-start.10 = (bf16[16,72,128]{2,1,0:T(8,128)(2,1)}, bf16[16,72,128]{2,1,0:T(8,128)(2,1)}, u32[]{:S(2)}, u32[]{:S(2)}) collective-permute-start(bf16[16,72,128]{2,1,0:T(8,128)(2,1)} %pad_maximum_fusion), channel_id=1, source_target_pairs={{32,0},{40,8},{48,16},{56,24},{64,32},{72,40},{80,48},{88,56},{96,... | collective-permute-start | bytes 884744 | tf_op jit(solution)/shard_map/ppermute | solution.py:16
  296.3 17.6 %collective-permute-start.9 = (bf16[16,72,128]{2,1,0:T(8,128)(2,1)}, bf16[16,72,128]{2,1,0:T(8,128)(2,1)}, u32[]{:S(2)}, u32[]{:S(2)}) collective-permute-start(bf16[16,72,128]{2,1,0:T(8,128)(2,1)} %pad_maximum_fusion), channel_id=1, source_target_pairs={{24,0},{32,8},{40,16},{48,24},{56,32},{64,40},{72,48},{80,56},{88,... | collective-permute-start | bytes 884744 | tf_op jit(solution)/shard_map/ppermute | solution.py:16
  319.2 15.3 %collective-permute-start.11 = (bf16[16,72,128]{2,1,0:T(8,128)(2,1)}, bf16[16,72,128]{2,1,0:T(8,128)(2,1)}, u32[]{:S(2)}, u32[]{:S(2)}) collective-permute-start(bf16[16,72,128]{2,1,0:T(8,128)(2,1)} %pad_maximum_fusion.3), channel_id=1, source_target_pairs={{32,0},{40,8},{48,16},{56,24},{64,32},{72,40},{80,48},{88,56},{96,... | collective-permute-start | bytes 884744 | tf_op jit(solution)/shard_map/ppermute | solution.py:16
  320.5 19.5 %collective-permute-start.12 = (bf16[16,72,128]{2,1,0:T(8,128)(2,1)}, bf16[16,72,128]{2,1,0:T(8,128)(2,1)}, u32[]{:S(2)}, u32[]{:S(2)}) collective-permute-start(bf16[16,72,128]{2,1,0:T(8,128)(2,1)} %pad_maximum_fusion.3), channel_id=1, source_target_pairs={{64,0},{72,8},{80,16},{88,24},{96,32},{104,40},{112,48},{120,56},{... | collective-permute-start | bytes 884744 | tf_op jit(solution)/shard_map/ppermute | solution.py:16
  324.1 50.0 %all-to-all-start = ((bf16[256,8,512]{2,0,1:T(8,128)(2,1)}), bf16[256,8,512]{2,0,1:T(8,128)(2,1)S(1)}, u32[]{:S(2)}, u32[]{:S(2)}) async-start(bf16[256,8,512]{2,0,1:T(8,128)(2,1)} %bitcast.123), calls=%async_computation | async-start | bytes 4194304 | tf_op jit(solution)/shard_map/all_to_all | solution.py:69
  328.7 28.6 %copy-start.22 = (f32[16,2]{0,1:T(2,128)S(1)}, f32[16,2]{0,1:T(2,128)}, u32[]{:S(2)}) copy-start(f32[16,2]{0,1:T(2,128)} %copy-done.21) | copy-start | bytes 388
  328.7 28.6 %copy-start.24 = (f32[256]{0:T(256)S(1)}, f32[256]{0:T(256)}, u32[]{:S(2)}) copy-start(f32[256]{0:T(256)} %copy-done.23) | copy-start | bytes 3076
  328.7 28.6 %copy-start.27 = (f32[16]{0:T(128)S(1)}, f32[16]{0:T(128)}, u32[]{:S(2)}) copy-start(f32[16]{0:T(128)} %copy-done.26) | copy-start | bytes 196
  328.7 34.9 %copy-start.15 = (f32[256,16]{0,1:T(8,128)S(1)}, f32[256,16]{0,1:T(8,128)}, u32[]{:S(2)}) copy-start(f32[256,16]{0,1:T(8,128)} %copy-done.14) | copy-start | bytes 49156
  328.7 34.9 %copy-start.17 = (pred[256,256]{1,0:T(8,128)(4,1)S(1)}, pred[256,256]{1,0:T(8,128)(4,1)}, u32[]{:S(2)}) copy-start(pred[256,256]{1,0:T(8,128)(4,1)} %copy-done.16) | copy-start | bytes 196612
  328.7 24.1 %collective-permute-start.13 = (bf16[16,72,128]{2,1,0:T(8,128)(2,1)}, bf16[16,72,128]{2,1,0:T(8,128)(2,1)S(1)}, u32[]{:S(2)}, u32[]{:S(2)}) collective-permute-start(bf16[16,72,128]{2,1,0:T(8,128)(2,1)} %pad_maximum_fusion.3), channel_id=1, source_target_pairs={{96,0},{104,8},{112,16},{120,24},{97,1},{105,9},{113,17},{121,25},... | collective-permute-start | bytes 884744 | tf_op jit(solution)/shard_map/ppermute | solution.py:16
  (24 other events, 300.8 us)
Sparse Core Ops, SparseCore 0:
  102.2 102.8 reduce-scatter.1
  207.6 71.5 all-gather.1

commit v4 on v3

--- a/solution.py
+++ b/solution.py
@@ -177,8 +177,20 @@
     weight_term = lax.dot_general(
         grad_full, normed_bf, (((0,), (0,)), ((), ())), preferred_element_type=jnp.float32
     ).astype(jnp.bfloat16)
+    seq_count = lax.axis_size("seq")
+    parity = lax.axis_index("seq") % 2
+    blocks = weight_term.reshape(seq_count // 2, 2, -1, weight_term.shape[1])
+    mine = lax.dynamic_index_in_dim(blocks, parity, axis=1, keepdims=False)
+    theirs = lax.dynamic_index_in_dim(blocks, 1 - parity, axis=1, keepdims=False)
+    partner = lax.ppermute(theirs, "seq", [(peer, peer ^ 1) for peer in range(seq_count)])
+    pair_sum = (mine.astype(jnp.float32) + partner.astype(jnp.float32)).astype(jnp.bfloat16)
+    groups = [list(range(start, seq_count, 2)) for start in range(2)]
     grad_weight = lax.psum_scatter(
-        weight_term, "seq", scatter_dimension=0, tiled=True
+        pair_sum.reshape(-1, weight_term.shape[1]),
+        "seq",
+        scatter_dimension=0,
+        tiled=True,
+        axis_index_groups=groups,
     ).astype(jnp.float32)
     after_term = grad_full + weight_term[0, 0] * jnp.zeros((), jnp.bfloat16)
     grad_y = jnp.dot(after_term, full_weight, preferred_element_type=jnp.float32)

time: 384 us -> 427 us (1.11)
  local copies, waits for them, and re-layouts: 21.8 us -> 93.3 us
  waiting for transfers between devices: 221 us -> 166 us
  other arithmetic: 33.6 us -> 51.3 us
    all_gather x1, waiting for transfers between devices: 71.8 us -> 0.01 us  [per_device(): full_weight = lax.all_gather(out_weight, 'seq', axis=0, tiled=True)]
    unnamed x79 -> x76, local copies, waits for them, and re-layouts: 6.17 us -> 44.9 us
    dynamic_slice x0 -> x1, local copies, waits for them, and re-layouts: none -> 20.3 us  [per_device(): mine = lax.dynamic_index_in_dim(blocks, parity, axis=1, keepdims=False)]
    reshape x0 -> x1, local copies, waits for them, and re-layouts: none -> 14.5 us  [per_device(): blocks = weight_term.reshape(seq_count // 2, 2, -1, weight_term.shape[1])]
    convert_element_type x0 -> x2, other arithmetic: none -> 9.85 us  [the longest x1 7.73 us: per_device(): (mine.astype(jnp.float32) + partner.astype(jnp.float32)).astype(jnp.bfloa...]
    reduce_scatter x1, waiting for transfers between devices: 100 us -> 110 us  [per_device(): lax.psum_scatter(pair_sum.reshape(-1, weight_term.shape[1]), 'seq', scatt...]
    ppermute x14, waiting for transfers between devices: 47.8 us -> 55.4 us  [from_behind(): lax.ppermute(value, axis, [(source, source + steps) for source in range(l...]
  transfers between devices with their start and end apart: 18 -> 19, of which waited for: 8 -> 6; matrix products, arithmetic and copies ran while one was open for 15% -> 23% of each run, Pallas kernels for 0% -> 0%
where the time goes in v4:
time: 427 us; the launch traced here: 423 us
  waiting for transfers between devices  166 us (39%)
  local copies, waits for them, and re-layouts  93.3 us (22%)
  other arithmetic  51.3 us (12%)
  starting transfers between devices  49.8 us (12%)
  matrix products  44.9 us (11%)
  between operations  17.5 us (4%)
    reduce_scatter x1, waiting for transfers between devices, per_device(): lax.psum_scatter(pair_sum.reshape(-1, weight_term.shape[1]), 'seq', scatt...  110 us
    ppermute x14, waiting for transfers between devices, from_behind(): lax.ppermute(value, axis, [(source, source + steps) for source in range(l...  55.4 us
    unnamed x76, local copies, waits for them, and re-layouts  44.9 us
    ppermute x14, starting transfers between devices, from_behind(): lax.ppermute(value, axis, [(source, source + steps) for source in range(l...  39.8 us
    dynamic_slice x1, local copies, waits for them, and re-layouts, per_device(): mine = lax.dynamic_index_in_dim(blocks, parity, axis=1, keepdims=False)  20.3 us
    reshape x1, local copies, waits for them, and re-layouts, per_device(): blocks = weight_term.reshape(seq_count // 2, 2, -1, weight_term.shape[1])  14.5 us
    dot_general x3, matrix products, block_outputs(): jnp.einsum('hts,shp->thp', scores, x_heads, precision=lax.Precision.HIGH)  14.2 us
    another operation x11, other arithmetic  9.32 us
  transfers between devices with their start and end apart: 19, of which 6 were waited for; matrix products, arithmetic and copies ran while one was open for 23% of the time, Pallas kernels for 0%

profile of v4, /device:TPU:0, one launch (start us, length us, event | category | flops | bytes accessed | tf_op | source)
XLA Modules:
  0.0 422.8 jit_solution(14054158069086753164)
XLA Ops:
  21.4 4.8 %collective-permute-start.1 = (bf16[16,72,128]{2,1,0:T(8,128)(2,1)}, bf16[16,72,128]{2,1,0:T(8,128)(2,1)}, u32[]{:S(2)}, u32[]{:S(2)}) collective-permute-start(bf16[16,72,128]{2,1,0:T(8,128)(2,1)} %pad_maximum_fusion.1), channel_id=1, source_target_pairs={{0,16},{8,24},{16,32},{24,40},{32,48},{40,56},{48,64},{56,72},{64,... | collective-permute-start | bytes 884744 | tf_op jit(solution)/shard_map/ppermute | solution.py:16
  26.2 4.7 %collective-permute-start.3 = (bf16[16,72,128]{2,1,0:T(8,128)(2,1)}, bf16[16,72,128]{2,1,0:T(8,128)(2,1)}, u32[]{:S(2)}, u32[]{:S(2)}) collective-permute-start(bf16[16,72,128]{2,1,0:T(8,128)(2,1)} %pad_maximum_fusion.1), channel_id=1, source_target_pairs={{0,32},{8,40},{16,48},{24,56},{32,64},{40,72},{48,80},{56,88},{64,... | collective-permute-start | bytes 884744 | tf_op jit(solution)/shard_map/ppermute | solution.py:16
  30.9 5.8 %collective-permute-start.2 = (bf16[16,72,128]{2,1,0:T(8,128)(2,1)}, bf16[16,72,128]{2,1,0:T(8,128)(2,1)}, u32[]{:S(2)}, u32[]{:S(2)}) collective-permute-start(bf16[16,72,128]{2,1,0:T(8,128)(2,1)} %pad_maximum_fusion.1), channel_id=1, source_target_pairs={{0,24},{8,32},{16,40},{24,48},{32,56},{40,64},{48,72},{56,80},{64,... | collective-permute-start | bytes 884744 | tf_op jit(solution)/shard_map/ppermute | solution.py:16
  36.7 2.5 broadcast_in_dim.22
  39.2 5.4 %all-to-all-start.1 = ((bf16[256,8,512]{2,0,1:T(8,128)(2,1)}), bf16[256,8,512]{2,0,1:T(8,128)(2,1)S(1)}, u32[]{:S(2)}, u32[]{:S(2)}) async-start(bf16[256,8,512]{2,0,1:T(8,128)(2,1)} %broadcast_in_dim.22), calls=%async_computation.1 | async-start | bytes 4194304 | tf_op jit(solution)/shard_map/all_to_all | solution.py:61
  47.8 2.3 fusion.107
  50.8 8.8 %collective-permute-start.5 = (bf16[16,72,128]{2,1,0:T(8,128)(2,1)}, bf16[16,72,128]{2,1,0:T(8,128)(2,1)S(1)}, u32[]{:S(2)}, u32[]{:S(2)}) collective-permute-start(bf16[16,72,128]{2,1,0:T(8,128)(2,1)} %pad_maximum_fusion.2), channel_id=1, source_target_pairs={{0,64},{8,72},{16,80},{24,88},{32,96},{40,104},{48,112},{56,120},{... | collective-permute-start | bytes 884744 | tf_op jit(solution)/shard_map/ppermute | solution.py:16
  59.6 3.6 collective-permute-start.4
  65.6 20.7 %collective-permute-done.5 = bf16[16,72,128]{2,1,0:T(8,128)(2,1)S(1)} collective-permute-done((bf16[16,72,128]{2,1,0:T(8,128)(2,1)}, bf16[16,72,128]{2,1,0:T(8,128)(2,1)S(1)}, u32[]{:S(2)}, u32[]{:S(2)}) %collective-permute-start.5) | collective-permute-done | bytes 294944 | tf_op jit(solution)/shard_map/ppermute | solution.py:16
  90.0 4.6 %fusion.33 = f32[256,16,64]{0,2,1:T(8,128)} fusion(bf16[256,16,64]{0,2,1:T(8,128)(2,1)S(1)} %bitcast.133, f32[16,256]{1,0:T(8,128)} %copy-done.18, f32[256,256]{1,0:T(8,128)} %fusion.114, pred[256,256]{1,0:T(8,128)(4,1)S(1)} %fusion.68, f32[256,16,64]{0,2,1:T(8,128)S(1)} %convolution_bitcast_fusion.1, f32[256,16]{0,1:T(8,128)} %get-tuple-element.169), kind=kOutput, calls=%fused_computation.39 | convolution fusion | flops 407371776 | bytes 2981888 | tf_op jit(solution)/shard_map/jvp(hts,shp->thp)/dot_general | solution.py:95
  98.7 2.4 copy.77
  101.1 7.7 %convert_bitcast_fusion = bf16[4096,1024]{0,1:T(8,128)(2,1)} fusion(bf16[256,4096]{0,1:T(8,128)(2,1)} %bitcast.137, f32[1024]{0:T(1024)} %param.31, f32[256]{0:T(256)} %fusion.92, f32[256,1024]{1,0:T(8,128)S(1)} %copy.75, bf16[256,1024]{1,0:T(8,128)(2,1)} %param.28), kind=kOutput, calls=%fused_computation.2 | convolution fusion | flops 2154037248 | bytes 12063744 | tf_op jit(solution)/shard_map/dot_general | solution.py:177
  108.9 14.5 %reshape.726 = bf16[8,2,256,1024]{2,1,0,3:T(2,128)(2,1)} reshape(bf16[4096,1024]{0,1:T(8,128)(2,1)} %convert_bitcast_fusion) | data formatting | bytes 16777216 | tf_op jit(solution)/shard_map/reshape | solution.py:182
  123.4 20.3 %constant_dynamic-slice_fusion.1 = (bf16[8,1,256,1024]{2,1,0,3:T(2,128)(2,1)}, bf16[8,1,256,1024]{2,1,0,3:T(2,128)(2,1)}) fusion(bf16[8,2,256,1024]{2,1,0,3:T(2,128)(2,1)} %reshape.726, s32[]{:T(128)S(6)} %select_n.33, s32[]{:T(128)S(6)} %select_n.34), kind=kLoop, calls=%fused_computation.168 | loop fusion | bytes 16777224 | tf_op jit(solution)/shard_map/jit(dynamic_index_in_dim)/dynamic_slice | solution.py:183
  143.7 20.0 %copy.89 = bf16[8,1,256,1024]{3,2,0,1:T(8,128)(2,1)} copy(bf16[8,1,256,1024]{2,1,0,3:T(2,128)(2,1)} %get-tuple-element.164) | data formatting | bytes 8388608
  163.7 20.0 %copy.88 = bf16[8,1,256,1024]{3,2,0,1:T(8,128)(2,1)} copy(bf16[8,1,256,1024]{2,1,0,3:T(2,128)(2,1)} %get-tuple-element.163) | data formatting | bytes 8388608
  183.8 7.7 %fusion = bf16[8,256,1024]{2,1,0:T(8,128)(2,1)} fusion(bf16[8,256,1024]{2,1,0:T(8,128)(2,1)} %collective-permute-done.14, bf16[8,1,256,1024]{3,2,0,1:T(8,128)(2,1)} %copy.88), kind=kLoop, calls=%fused_computation.1 | loop fusion | flops 8388608 | bytes 12582912 | tf_op jit(solution)/shard_map/convert_element_type | solution.py:186
  194.0 110.1 %reduce-scatter.2.cloned.1.call-done = bf16[256,1024]{1,0:T(8,128)(2,1)} async-done(((bf16[2048,1024]{1,0:T(8,128)(2,1)}), bf16[256,1024]{1,0:T(8,128)(2,1)}) %reduce-scatter.2.cloned.1.call-update) | async-done | bytes 524304 | tf_op jit(solution)/shard_map/reduce_scatter | solution.py:188
  306.2 6.0 %convolution_convert_fusion = bf16[256,4096]{1,0:T(8,128)(2,1)S(1)} fusion(bf16[4096,1024]{1,0:T(8,128)(2,1)} %all-gather.2.cloned.1.call-done, f32[1024]{0:T(1024)S(1)} %copy-done.35, f32[256]{0:T(256)S(1)} %copy-done.32, f32[256,1024]{1,0:T(8,128)S(1)} %copy.75, bf16[256,1024]{1,0:T(8,128)(2,1)S(1)} %copy-done.6), kind=kOutput, calls=%fused_computation.6 | convolution fusion | flops 2150891520 | bytes 12063744 | tf_op jit(solution)/shard_map/dot_general | solution.py:172
  313.7 4.5 %all-to-all-start = ((bf16[256,8,512]{2,0,1:T(8,128)(2,1)}), bf16[256,8,512]{2,0,1:T(8,128)(2,1)S(1)}, u32[]{:S(2)}, u32[]{:S(2)}) async-start(bf16[256,8,512]{2,0,1:T(8,128)(2,1)} %bitcast.131), calls=%async_computation | async-start | bytes 4194304 | tf_op jit(solution)/shard_map/all_to_all | solution.py:69
  318.3 6.7 %multiply_reduce_fusion.1 = (f32[256]{0:T(256)S(1)}, f32[256,1024]{1,0:T(8,128)S(1)}) fusion(f32[256,1024]{1,0:T(8,128)S(1)} %copy.75, bf16[256,1024]{1,0:T(8,128)(2,1)} %param.28, f32[1024]{0:T(1024)} %param.31, bf16[4096,1024]{1,0:T(8,128)(2,1)} %all-gather.2.cloned.1.call-done, bf16[256,4096]{0,1:T(8,128)(2,1)} %bitcast.138, bf16[]{:T(256)} %bitcast.11), kind=kOutput, calls=%fused_computation.60 | convolution fusion | flops 2150891264 | bytes 13112322 | tf_op jit(solution)/shard_map/dot_general | solution.py:196
  331.4 5.5 %fusion.61 = (f32[16,256]{1,0:T(8,128)S(1)}, f32[16,256]{1,0:T(8,128)S(1)}, f32[256,256]{1,0:T(8,128)S(1)}) fusion(f32[16,256]{1,0:T(8,128)} %copy-done.18, f32[256,256]{1,0:T(8,128)} %fusion.114, pred[256,256]{1,0:T(8,128)(4,1)} %copy-done.17, f32[16,64,256]{2,1,0:T(8,128)S(1)} %bitcast.128, bf16[256,16,64]{0,2,1:T(8,128)(2,1)} %bitcast.134), kind=kOutput, calls=%fused_computation.71 | convolution fusion | flops 418308096 | bytes 2211840 | tf_op jit(solution)/shard_map/transpose(jvp(hts,shp->thp))/dot_general | solution.py:95
  344.4 2.5 reduce-window.41
  348.0 7.2 %collective-permute-done.8 = bf16[16,72,128]{2,1,0:T(8,128)(2,1)} collective-permute-done((bf16[16,72,128]{2,1,0:T(8,128)(2,1)}, bf16[16,72,128]{2,1,0:T(8,128)(2,1)}, u32[]{:S(2)}, u32[]{:S(2)}) %collective-permute-start.8) | collective-permute-done | bytes 294944 | tf_op jit(solution)/shard_map/ppermute | solution.py:16
  357.6 2.3 fusion.100
  366.4 17.0 %collective-permute-done.12 = bf16[16,72,128]{2,1,0:T(8,128)(2,1)} collective-permute-done((bf16[16,72,128]{2,1,0:T(8,128)(2,1)}, bf16[16,72,128]{2,1,0:T(8,128)(2,1)}, u32[]{:S(2)}, u32[]{:S(2)}) %collective-permute-start.12) | collective-permute-done | bytes 294944 | tf_op jit(solution)/shard_map/ppermute | solution.py:16
  385.5 9.4 %collective-permute-done.13 = bf16[16,72,128]{2,1,0:T(8,128)(2,1)S(1)} collective-permute-done((bf16[16,72,128]{2,1,0:T(8,128)(2,1)}, bf16[16,72,128]{2,1,0:T(8,128)(2,1)S(1)}, u32[]{:S(2)}, u32[]{:S(2)}) %collective-permute-start.13) | collective-permute-done | bytes 294944 | tf_op jit(solution)/shard_map/ppermute | solution.py:16
  398.5 4.1 fusion.36
  402.6 2.5 copy.87
  405.5 2.5 reduce-window.49
  408.1 2.5 reduce-window.45
  411.5 2.9 fusion.44
  (185 shorter events, 63.7 us)
Async XLA Ops:
  17.6 72.3 %copy-start = (bf16[256,1024]{0,1:T(8,128)(2,1)}, bf16[256,1024]{0,1:T(8,128)(2,1)S(1)}, u32[]{:S(2)}) copy-start(bf16[256,1024]{0,1:T(8,128)(2,1)S(1)} %copy.74) | copy-start | bytes 1572868
  17.9 32.1 %copy-start.10 = (bf16[16,8,128]{2,1,0:T(8,128)(2,1)}, bf16[16,8,128]{2,1,0:T(8,128)(2,1)S(1)}, u32[]{:S(2)}) copy-start(bf16[16,8,128]{2,1,0:T(8,128)(2,1)S(1)} %scatter.21) | copy-start | bytes 98308
  18.6 31.5 %copy-start.15 = (f32[256,16]{0,1:T(8,128)}, f32[256,16]{0,1:T(8,128)S(1)}, u32[]{:S(2)}) copy-start(f32[256,16]{0,1:T(8,128)S(1)} %get-tuple-element.170) | copy-start | bytes 49156
  19.9 43.2 %copy-start.8 = (bf16[256,128]{1,0:T(8,128)(2,1)S(1)}, bf16[256,128]{1,0:T(8,128)(2,1)}, u32[]{:S(2)}) copy-start(bf16[256,128]{1,0:T(8,128)(2,1)} %param.26) | copy-start | bytes 196612
  19.9 43.2 %copy-start.9 = (bf16[256,128]{1,0:T(8,128)(2,1)S(1)}, bf16[256,128]{1,0:T(8,128)(2,1)}, u32[]{:S(2)}) copy-start(bf16[256,128]{1,0:T(8,128)(2,1)} %param.27) | copy-start | bytes 196612
  19.9 24.7 %collective-permute-start = (bf16[16,72,128]{2,1,0:T(8,128)(2,1)}, bf16[16,72,128]{2,1,0:T(8,128)(2,1)S(1)}, u32[]{:S(2)}, u32[]{:S(2)}) collective-permute-start(bf16[16,72,128]{2,1,0:T(8,128)(2,1)} %pad_maximum_fusion.1), channel_id=1, source_target_pairs={{0,8},{8,16},{16,24},{24,32},{32,40},{40,48},{48,56},{56,64},{64,7... | collective-permute-start | bytes 884744 | tf_op jit(solution)/shard_map/ppermute | solution.py:16
  21.4 23.5 %collective-permute-start.1 = (bf16[16,72,128]{2,1,0:T(8,128)(2,1)}, bf16[16,72,128]{2,1,0:T(8,128)(2,1)}, u32[]{:S(2)}, u32[]{:S(2)}) collective-permute-start(bf16[16,72,128]{2,1,0:T(8,128)(2,1)} %pad_maximum_fusion.1), channel_id=1, source_target_pairs={{0,16},{8,24},{16,32},{24,40},{32,48},{40,56},{48,64},{56,72},{64,... | collective-permute-start | bytes 884744 | tf_op jit(solution)/shard_map/ppermute | solution.py:16
  26.2 19.7 %collective-permute-start.3 = (bf16[16,72,128]{2,1,0:T(8,128)(2,1)}, bf16[16,72,128]{2,1,0:T(8,128)(2,1)}, u32[]{:S(2)}, u32[]{:S(2)}) collective-permute-start(bf16[16,72,128]{2,1,0:T(8,128)(2,1)} %pad_maximum_fusion.1), channel_id=1, source_target_pairs={{0,32},{8,40},{16,48},{24,56},{32,64},{40,72},{48,80},{56,88},{64,... | collective-permute-start | bytes 884744 | tf_op jit(solution)/shard_map/ppermute | solution.py:16
  30.9 15.0 %collective-permute-start.2 = (bf16[16,72,128]{2,1,0:T(8,128)(2,1)}, bf16[16,72,128]{2,1,0:T(8,128)(2,1)}, u32[]{:S(2)}, u32[]{:S(2)}) collective-permute-start(bf16[16,72,128]{2,1,0:T(8,128)(2,1)} %pad_maximum_fusion.1), channel_id=1, source_target_pairs={{0,24},{8,32},{16,40},{24,48},{32,56},{40,64},{48,72},{56,80},{64,... | collective-permute-start | bytes 884744 | tf_op jit(solution)/shard_map/ppermute | solution.py:16
  39.2 59.6 %all-to-all-start.1 = ((bf16[256,8,512]{2,0,1:T(8,128)(2,1)}), bf16[256,8,512]{2,0,1:T(8,128)(2,1)S(1)}, u32[]{:S(2)}, u32[]{:S(2)}) async-start(bf16[256,8,512]{2,0,1:T(8,128)(2,1)} %broadcast_in_dim.22), calls=%async_computation.1 | async-start | bytes 4194304 | tf_op jit(solution)/shard_map/all_to_all | solution.py:61
  44.6 259.5 %reduce-scatter.2.cloned.1.call-start = ((), (), s32[]{:S(2)}) async-start(), calls=%async_computation.4 | async-start | bytes 4718592 | tf_op jit(solution)/shard_map/reduce_scatter | solution.py:188
  50.8 35.4 %collective-permute-start.5 = (bf16[16,72,128]{2,1,0:T(8,128)(2,1)}, bf16[16,72,128]{2,1,0:T(8,128)(2,1)S(1)}, u32[]{:S(2)}, u32[]{:S(2)}) collective-permute-start(bf16[16,72,128]{2,1,0:T(8,128)(2,1)} %pad_maximum_fusion.2), channel_id=1, source_target_pairs={{0,64},{8,72},{16,80},{24,88},{32,96},{40,104},{48,112},{56,120},{... | collective-permute-start | bytes 884744 | tf_op jit(solution)/shard_map/ppermute | solution.py:16
  59.6 26.6 %collective-permute-start.4 = (bf16[16,72,128]{2,1,0:T(8,128)(2,1)}, bf16[16,72,128]{2,1,0:T(8,128)(2,1)}, u32[]{:S(2)}, u32[]{:S(2)}) collective-permute-start(bf16[16,72,128]{2,1,0:T(8,128)(2,1)} %pad_maximum_fusion.2), channel_id=1, source_target_pairs={{0,32},{8,40},{16,48},{24,56},{32,64},{40,72},{48,80},{56,88},{64,... | collective-permute-start | bytes 884744 | tf_op jit(solution)/shard_map/ppermute | solution.py:16
  64.1 23.1 %collective-permute-start.6 = (bf16[16,72,128]{2,1,0:T(8,128)(2,1)}, bf16[16,72,128]{2,1,0:T(8,128)(2,1)S(1)}, u32[]{:S(2)}, u32[]{:S(2)}) collective-permute-start(bf16[16,72,128]{2,1,0:T(8,128)(2,1)} %pad_maximum_fusion.2), channel_id=1, source_target_pairs={{0,96},{8,104},{16,112},{24,120},{1,97},{9,105},{17,113},{25,121},... | collective-permute-start | bytes 884744 | tf_op jit(solution)/shard_map/ppermute | solution.py:16
  65.5 29.0 %copy-start.17 = (pred[256,256]{1,0:T(8,128)(4,1)}, pred[256,256]{1,0:T(8,128)(4,1)S(1)}, u32[]{:S(2)}) copy-start(pred[256,256]{1,0:T(8,128)(4,1)S(1)} %fusion.68) | copy-start | bytes 196612
  163.7 20.1 %collective-permute-start.14 = (bf16[8,256,1024]{2,1,0:T(8,128)(2,1)}, bf16[8,256,1024]{2,1,0:T(8,128)(2,1)}, u32[]{:S(2)}, u32[]{:S(2)}) collective-permute-start(bf16[8,256,1024]{2,1,0:T(8,128)(2,1)} %bitcast.136), channel_id=1, source_target_pairs={{0,8},{8,0},{16,24},{24,16},{32,40},{40,32},{48,56},{56,48},{64,72... | collective-permute-start | bytes 12582920 | tf_op jit(solution)/shard_map/ppermute | solution.py:185
  191.5 114.7 %copy-start.6 = (bf16[256,1024]{1,0:T(8,128)(2,1)S(1)}, bf16[256,1024]{1,0:T(8,128)(2,1)}, u32[]{:S(2)}) copy-start(bf16[256,1024]{1,0:T(8,128)(2,1)} %param.28) | copy-start | bytes 1572868
  191.5 114.7 %copy-start.32 = (f32[256]{0:T(256)S(1)}, f32[256]{0:T(256)}, u32[]{:S(2)}) copy-start(f32[256]{0:T(256)} %fusion.92) | copy-start | bytes 3076
  191.5 114.7 %copy-start.35 = (f32[1024]{0:T(1024)S(1)}, f32[1024]{0:T(1024)}, u32[]{:S(2)}) copy-start(f32[1024]{0:T(1024)} %param.31) | copy-start | bytes 12292
  191.5 114.7 %all-gather.2.cloned.1.call-start = ((), (), s32[]{:S(2)}) async-start(), calls=%async_computation.3 | async-start | bytes 8912896 | tf_op jit(solution)/shard_map/all_gather | solution.py:171
  313.7 100.6 %all-to-all-start = ((bf16[256,8,512]{2,0,1:T(8,128)(2,1)}), bf16[256,8,512]{2,0,1:T(8,128)(2,1)S(1)}, u32[]{:S(2)}, u32[]{:S(2)}) async-start(bf16[256,8,512]{2,0,1:T(8,128)(2,1)} %bitcast.131), calls=%async_computation | async-start | bytes 4194304 | tf_op jit(solution)/shard_map/all_to_all | solution.py:69
  338.9 8.0 %collective-permute-start.7 = (bf16[16,72,128]{2,1,0:T(8,128)(2,1)}, bf16[16,72,128]{2,1,0:T(8,128)(2,1)}, u32[]{:S(2)}, u32[]{:S(2)}) collective-permute-start(bf16[16,72,128]{2,1,0:T(8,128)(2,1)} %pad_maximum_fusion), channel_id=1, source_target_pairs={{8,0},{16,8},{24,16},{32,24},{40,32},{48,40},{56,48},{64,56},{72,6... | collective-permute-start | bytes 884744 | tf_op jit(solution)/shard_map/ppermute | solution.py:16
  340.5 15.7 %collective-permute-start.10 = (bf16[16,72,128]{2,1,0:T(8,128)(2,1)}, bf16[16,72,128]{2,1,0:T(8,128)(2,1)}, u32[]{:S(2)}, u32[]{:S(2)}) collective-permute-start(bf16[16,72,128]{2,1,0:T(8,128)(2,1)} %pad_maximum_fusion), channel_id=1, source_target_pairs={{32,0},{40,8},{48,16},{56,24},{64,32},{72,40},{80,48},{88,56},{96,... | collective-permute-start | bytes 884744 | tf_op jit(solution)/shard_map/ppermute | solution.py:16
  341.8 14.4 %collective-permute-start.9 = (bf16[16,72,128]{2,1,0:T(8,128)(2,1)}, bf16[16,72,128]{2,1,0:T(8,128)(2,1)}, u32[]{:S(2)}, u32[]{:S(2)}) collective-permute-start(bf16[16,72,128]{2,1,0:T(8,128)(2,1)} %pad_maximum_fusion), channel_id=1, source_target_pairs={{24,0},{32,8},{40,16},{48,24},{56,32},{64,40},{72,48},{80,56},{88,... | collective-permute-start | bytes 884744 | tf_op jit(solution)/shard_map/ppermute | solution.py:16
  343.1 12.1 %collective-permute-start.8 = (bf16[16,72,128]{2,1,0:T(8,128)(2,1)}, bf16[16,72,128]{2,1,0:T(8,128)(2,1)}, u32[]{:S(2)}, u32[]{:S(2)}) collective-permute-start(bf16[16,72,128]{2,1,0:T(8,128)(2,1)} %pad_maximum_fusion), channel_id=1, source_target_pairs={{16,0},{24,8},{32,16},{40,24},{48,32},{56,40},{64,48},{72,56},{80,... | collective-permute-start | bytes 884744 | tf_op jit(solution)/shard_map/ppermute | solution.py:16
  357.5 40.9 %copy-start.16 = (f32[256,16]{0,1:T(8,128)S(1)}, f32[256,16]{0,1:T(8,128)}, u32[]{:S(2)}) copy-start(f32[256,16]{0,1:T(8,128)} %copy-done.15) | copy-start | bytes 49156
  357.6 40.9 %copy-start.19 = (f32[16,256]{1,0:T(8,128)S(1)}, f32[16,256]{1,0:T(8,128)}, u32[]{:S(2)}) copy-start(f32[16,256]{1,0:T(8,128)} %copy-done.18) | copy-start | bytes 49156
  360.6 22.8 %collective-permute-start.12 = (bf16[16,72,128]{2,1,0:T(8,128)(2,1)}, bf16[16,72,128]{2,1,0:T(8,128)(2,1)}, u32[]{:S(2)}, u32[]{:S(2)}) collective-permute-start(bf16[16,72,128]{2,1,0:T(8,128)(2,1)} %pad_maximum_fusion.3), channel_id=1, source_target_pairs={{64,0},{72,8},{80,16},{88,24},{96,32},{104,40},{112,48},{120,56},{... | collective-permute-start | bytes 884744 | tf_op jit(solution)/shard_map/ppermute | solution.py:16
  361.9 22.5 %collective-permute-start.11 = (bf16[16,72,128]{2,1,0:T(8,128)(2,1)}, bf16[16,72,128]{2,1,0:T(8,128)(2,1)}, u32[]{:S(2)}, u32[]{:S(2)}) collective-permute-start(bf16[16,72,128]{2,1,0:T(8,128)(2,1)} %pad_maximum_fusion.3), channel_id=1, source_target_pairs={{32,0},{40,8},{48,16},{56,24},{64,32},{72,40},{80,48},{88,56},{96,... | collective-permute-start | bytes 884744 | tf_op jit(solution)/shard_map/ppermute | solution.py:16
  363.3 33.8 %copy-start.1 = (bf16[256,1024]{0,1:T(8,128)(2,1)S(1)}, bf16[256,1024]{0,1:T(8,128)(2,1)}, u32[]{:S(2)}) copy-start(bf16[256,1024]{0,1:T(8,128)(2,1)} %copy-done) | copy-start | bytes 1572868
  363.3 35.1 %copy-start.13 = (f32[256,256]{1,0:T(8,128)S(1)}, f32[256,256]{1,0:T(8,128)}, u32[]{:S(2)}) copy-start(f32[256,256]{1,0:T(8,128)} %fusion.114) | copy-start | bytes 786436
  363.3 31.6 %collective-permute-start.13 = (bf16[16,72,128]{2,1,0:T(8,128)(2,1)}, bf16[16,72,128]{2,1,0:T(8,128)(2,1)S(1)}, u32[]{:S(2)}, u32[]{:S(2)}) collective-permute-start(bf16[16,72,128]{2,1,0:T(8,128)(2,1)} %pad_maximum_fusion.3), channel_id=1, source_target_pairs={{96,0},{104,8},{112,16},{120,24},{97,1},{105,9},{113,17},{121,25},... | collective-permute-start | bytes 884744 | tf_op jit(solution)/shard_map/ppermute | solution.py:16
  (23 other events, 205.8 us)
Sparse Core Ops, SparseCore 0:
  191.6 112.4 reduce-scatter.1
Sparse Core Ops, SparseCore 1:
  194.4 77.7 all-gather.1
